TPU v7x, 128 devices: a whole 4x4x4 slice. The times are simulated.
128 devices in a mesh: chan: 16 (over y_lo, z, core), hour: 8 (over y_hi, x).
Axes of the slice: x: 4, y: 4 (y_hi: 2, y_lo: 2; y = y_hi * 2 + y_lo), z: 4, core: 2. Of those that a mesh axis runs over, the one named last changes fastest.
Arguments:
- spectra: bfloat16 [64, 128, 4096], P('hour', 'chan'), may hold values from -200 to 200
- quality: int32 [128], P('chan'), may hold values 0 or 1
- plan: int32 [4], replicated, may hold values from 1 to 15, as said below
Outputs:
- correlations: float32 [4, 8, 128, 512], P(None, 'hour', 'chan')
Inputs may be any that keep to these rules, and one draw needn't show every extreme that they name: `plan`: distinct numbers; 1 and 15 are among them.
All inputs are finite; a program needn't handle non-finite values. No bound on the sum of `quality` on one device may be relied on, other than what follows from the above.
Results may differ from a plain program's by a relative error of at most 0.004.
Values may be sent and summed in bfloat16 or wider, within the bound.
No kernel may reach another device: no remote copies, remote signals or barrier semaphores. Data moves between devices by JAX's collectives and lax.ppermute only.
A program may use at most 320 MiB of HBM per device.

v0:
```python
import jax
import jax.numpy as jnp
from jax import lax
from jax.sharding import PartitionSpec as P

BAND = 64
LAGS = 512
ROUNDS = 4


def partner_2(value, axis, apart):
    return lax.ppermute(value, axis, [(i, i ^ 1 << apart) for i in range(lax.axis_size(axis))])


def whiten(spectra, quality):
    hours, chans, width = spectra.shape
    n_freq = width // 2
    values = spectra.astype(jnp.float32)
    real_part = values[..., :n_freq]
    imag_part = values[..., n_freq:]
    power_sum = real_part * real_part + imag_part * imag_part
    band_mean = jnp.mean(
        power_sum.reshape(hours, chans, n_freq // BAND, BAND), axis=-1, keepdims=True
    )
    gain_band = lax.rsqrt(band_mean + 1e-06)
    gain_full = jnp.broadcast_to(gain_band, (hours, chans, n_freq // BAND, BAND)).reshape(
        hours, chans, n_freq
    )
    gain_both = jnp.concatenate([gain_full, gain_full], axis=-1)
    scaled = values * gain_both * quality.astype(jnp.float32)[None, :, None]
    return scaled.astype(jnp.bfloat16)


def lag_table(n_freq, total_hours):
    freq_index = jnp.arange(n_freq, dtype=jnp.int32)[:, None]
    lag_index = jnp.arange(LAGS, dtype=jnp.int32)[None, :] - LAGS // 2
    phase_int = freq_index * lag_index % (2 * n_freq)
    angle = jnp.pi * phase_int.astype(jnp.float32) / n_freq
    factor = 1.0 / jnp.sqrt(jnp.float32(total_hours * n_freq))
    return jnp.concatenate([jnp.cos(angle), -jnp.sin(angle)], axis=0) * factor


def cross_spectrum(own_block, partner):
    n_freq = own_block.shape[2] // 2
    own_re = own_block[..., :n_freq]
    own_im = own_block[..., n_freq:]
    far_re = partner[..., :n_freq]
    far_im = partner[..., n_freq:]
    f32 = jnp.float32
    cross_re = jnp.einsum("hjf,hif->jif", far_re, own_re, preferred_element_type=f32) + jnp.einsum(
        "hjf,hif->jif", far_im, own_im, preferred_element_type=f32
    )
    cross_im = jnp.einsum("hjf,hif->jif", far_re, own_im, preferred_element_type=f32) - jnp.einsum(
        "hjf,hif->jif", far_im, own_re, preferred_element_type=f32
    )
    return jnp.concatenate([cross_re, cross_im], axis=-1)


def to_lags(cross_spec, weights):
    rows_far, rows_own, width = cross_spec.shape
    flat = cross_spec.reshape(rows_far * rows_own, width)
    lagged = jnp.dot(
        flat, weights, precision=lax.Precision.HIGHEST, preferred_element_type=jnp.float32
    )
    return lagged.reshape(rows_far, rows_own, weights.shape[1])


def per_device(spectra, quality, plan):
    hours, chans, width = spectra.shape
    n_freq = width // 2
    own_block = whiten(spectra, quality)
    weights = lag_table(n_freq, hours * lax.axis_size("hour"))
    bit_count = lax.axis_size("chan").bit_length() - 1
    results = []
    for rnd_index in range(ROUNDS):
        xor_mask = plan[rnd_index]
        partner = own_block
        for bit_pos in range(bit_count):
            moved = partner_2(partner, "chan", bit_pos)
            partner = jnp.where(
                jnp.bitwise_and(jnp.right_shift(xor_mask, bit_pos), 1) == 1, moved, partner
            )

        def term_rows(start, count, partner=partner):
            return to_lags(cross_spectrum(own_block, partner), weights)

        stacked = lax.psum_scatter(
            term_rows(jnp.int32(0), lax.axis_size("hour") * (chans // lax.axis_size("hour"))),
            "hour",
            scatter_dimension=0,
            tiled=True,
        )
        results.append(stacked)
    return jnp.stack(results)


def solution(mesh):
    return jax.shard_map(
        per_device,
        mesh=mesh,
        in_specs=(P("hour", "chan", None), P("chan"), P()),
        out_specs=P(None, "hour", "chan", None),
        check_vma=False,
    )
```

profile of v0, /device:TPU:0, one launch (start us, length us, event | category | flops | bytes accessed | tf_op | source)
XLA Modules:
  0.0 606.6 jit_solution(11774281974281043446)
XLA Ops:
  20.2 4.1 copy.7
  24.3 4.0 copy.4
  28.5 2.1 collective-permute-start.1
  30.6 17.9 %fusion.15 = (f32[2048,512]{1,0:T(8,128)}, f32[2048,512]{1,0:T(8,128)}) fusion(s32[512]{0:T(512)S(1)} %iota_add_fusion), kind=kLoop, calls=%fused_computation.16 | loop fusion | flops 15728640 | bytes 8390656 | tf_op jit(solution)/shard_map/cos | solution.py:40
  48.6 1.9 collective-permute-start.7
  50.7 3.9 collective-permute-start.2
  54.6 8.6 %collective-permute-done.4 = bf16[8,8,4096]{2,1,0:T(8,128)(2,1)S(1)} collective-permute-done((bf16[8,8,4096]{2,1,0:T(8,128)(2,1)S(1)}, bf16[8,8,4096]{2,1,0:T(8,128)(2,1)S(1)}, u32[]{:S(2)}, u32[]{:S(2)}) %collective-permute-start.4) | collective-permute-done | bytes 524320 | tf_op jit(solution)/shard_map/ppermute | solution.py:12
  63.3 3.7 collective-permute-start.5
  67.0 7.5 %collective-permute-done.7 = bf16[8,8,4096]{2,1,0:T(8,128)(2,1)S(1)} collective-permute-done((bf16[8,8,4096]{2,1,0:T(8,128)(2,1)S(1)}, bf16[8,8,4096]{2,1,0:T(8,128)(2,1)S(1)}, u32[]{:S(2)}, u32[]{:S(2)}) %collective-permute-start.7) | collective-permute-done | bytes 524320 | tf_op jit(solution)/shard_map/ppermute | solution.py:12
  74.5 3.7 collective-permute-start.8
  78.2 7.5 %collective-permute-done.10 = bf16[8,8,4096]{2,1,0:T(8,128)(2,1)S(1)} collective-permute-done((bf16[8,8,4096]{2,1,0:T(8,128)(2,1)S(1)}, bf16[8,8,4096]{2,1,0:T(8,128)(2,1)S(1)}, u32[]{:S(2)}, u32[]{:S(2)}) %collective-permute-start.10) | collective-permute-done | bytes 524320 | tf_op jit(solution)/shard_map/ppermute | solution.py:12
  85.8 3.7 collective-permute-start.11
  89.5 9.5 %collective-permute-done.2 = bf16[8,8,4096]{2,1,0:T(8,128)(2,1)S(1)} collective-permute-done((bf16[8,8,4096]{2,1,0:T(8,128)(2,1)S(1)}, bf16[8,8,4096]{2,1,0:T(8,128)(2,1)S(1)}, u32[]{:S(2)}, u32[]{:S(2)}) %collective-permute-start.2) | collective-permute-done | bytes 524320 | tf_op jit(solution)/shard_map/ppermute | solution.py:12
  100.6 9.5 %collective-permute-done.5 = bf16[8,8,4096]{2,1,0:T(8,128)(2,1)S(1)} collective-permute-done((bf16[8,8,4096]{2,1,0:T(8,128)(2,1)S(1)}, bf16[8,8,4096]{2,1,0:T(8,128)(2,1)S(1)}, u32[]{:S(2)}, u32[]{:S(2)}) %collective-permute-start.5) | collective-permute-done | bytes 524320 | tf_op jit(solution)/shard_map/ppermute | solution.py:12
  111.9 9.5 %collective-permute-done.8 = bf16[8,8,4096]{2,1,0:T(8,128)(2,1)S(1)} collective-permute-done((bf16[8,8,4096]{2,1,0:T(8,128)(2,1)S(1)}, bf16[8,8,4096]{2,1,0:T(8,128)(2,1)S(1)}, u32[]{:S(2)}, u32[]{:S(2)}) %collective-permute-start.8) | collective-permute-done | bytes 524320 | tf_op jit(solution)/shard_map/ppermute | solution.py:12
  123.1 8.8 %collective-permute-done.11 = bf16[8,8,4096]{2,1,0:T(8,128)(2,1)S(1)} collective-permute-done((bf16[8,8,4096]{2,1,0:T(8,128)(2,1)S(1)}, bf16[8,8,4096]{2,1,0:T(8,128)(2,1)S(1)}, u32[]{:S(2)}, u32[]{:S(2)}) %collective-permute-start.11) | collective-permute-done | bytes 524320 | tf_op jit(solution)/shard_map/ppermute | solution.py:12
  132.0 1.8 collective-permute-start.12
  133.9 4.0 copy.5
  137.9 4.0 copy.8
  141.9 9.2 %fusion.47 = f32[2048,8,8]{2,1,0:T(8,128)} fusion(bf16[8,8,2048]{0,1,2:T(8,128)(2,1)} %copy.7, bf16[8,8,2048]{1,0,2:T(8,128)(2,1)} %copy.5), kind=kOutput, calls=%fused_computation.78 | convolution fusion | flops 2097152 | bytes 1048576 | tf_op jit(solution)/shard_map/hjf,hif->jif/dot_general | solution.py:53
  151.1 5.6 fusion.45
  156.7 5.6 fusion.48
  162.2 5.6 fusion.46
  168.0 4.2 copy.12
  172.2 9.2 %fusion.49 = f32[2048,8,8]{2,1,0:T(8,128)} fusion(bf16[8,8,2048]{0,1,2:T(8,128)(2,1)} %copy.4, bf16[8,8,2048]{1,0,2:T(8,128)(2,1)} %copy.12), kind=kOutput, calls=%fused_computation.80 | convolution fusion | flops 2097152 | bytes 1048576 | tf_op jit(solution)/shard_map/hjf,hif->jif/dot_general | solution.py:50
  181.4 5.6 fusion.51
  186.9 4.0 copy.14
  190.9 9.2 %fusion.50 = f32[2048,8,8]{2,1,0:T(8,128)} fusion(bf16[8,8,2048]{0,1,2:T(8,128)(2,1)} %copy.7, bf16[8,8,2048]{1,0,2:T(8,128)(2,1)} %copy.14), kind=kOutput, calls=%fused_computation.81 | convolution fusion | flops 2097152 | bytes 1048576 | tf_op jit(solution)/shard_map/hjf,hif->jif/dot_general | solution.py:50
  200.1 5.6 fusion.52
  205.7 4.4 copy.20
  210.2 9.2 %fusion.54 = f32[2048,8,8]{2,1,0:T(8,128)} fusion(bf16[8,8,2048]{0,1,2:T(8,128)(2,1)} %copy.7, bf16[8,8,2048]{1,0,2:T(8,128)(2,1)} %copy.20), kind=kOutput, calls=%fused_computation.85 | convolution fusion | flops 2097152 | bytes 1048576 | tf_op jit(solution)/shard_map/hjf,hif->jif/dot_general | solution.py:50
  219.4 5.6 fusion.56
  225.0 4.0 copy.18
  229.0 9.2 %fusion.53 = f32[2048,8,8]{2,1,0:T(8,128)} fusion(bf16[8,8,2048]{0,1,2:T(8,128)(2,1)} %copy.4, bf16[8,8,2048]{1,0,2:T(8,128)(2,1)} %copy.18), kind=kOutput, calls=%fused_computation.84 | convolution fusion | flops 2097152 | bytes 1048576 | tf_op jit(solution)/shard_map/hjf,hif->jif/dot_general | solution.py:50
  238.2 5.6 fusion.55
  243.9 4.2 copy.26
  248.1 9.2 %fusion.58 = f32[2048,8,8]{2,1,0:T(8,128)} fusion(bf16[8,8,2048]{0,1,2:T(8,128)(2,1)} %copy.7, bf16[8,8,2048]{1,0,2:T(8,128)(2,1)} %copy.26), kind=kOutput, calls=%fused_computation.89 | convolution fusion | flops 2097152 | bytes 1048576 | tf_op jit(solution)/shard_map/hjf,hif->jif/dot_general | solution.py:50
  257.3 5.6 fusion.60
  262.9 4.0 copy.24
  266.9 9.2 %fusion.57 = f32[2048,8,8]{2,1,0:T(8,128)} fusion(bf16[8,8,2048]{0,1,2:T(8,128)(2,1)} %copy.4, bf16[8,8,2048]{1,0,2:T(8,128)(2,1)} %copy.24), kind=kOutput, calls=%fused_computation.88 | convolution fusion | flops 2097152 | bytes 1048576 | tf_op jit(solution)/shard_map/hjf,hif->jif/dot_general | solution.py:50
  276.1 5.5 fusion.59
  281.7 5.2 copy.10
  286.8 5.2 copy.11
  292.0 5.2 copy.6
  297.2 5.6 copy.9
  302.9 9.5 %fusion.13 = f32[8,8,512]{2,1,0:T(8,128)} fusion(f32[2048,512]{1,0:T(8,128)} %get-tuple-element.20, f32[2048,512]{1,0:T(8,128)} %get-tuple-element.19, f32[8,8,2048]{2,1,0:T(8,128)S(1)} %get-tuple-element.31, f32[8,8,2048]{2,1,0:T(8,128)S(1)} %get-tuple-element.32), kind=kOutput, calls=%fused_computation.15 | convolution fusion | flops 1615069184 | bytes 9568256 | tf_op jit(solution)/shard_map/dot_general | solution.py:62
  312.5 5.2 copy.13
  317.7 5.2 copy.15
  322.9 5.2 copy.16
  328.1 5.2 copy.17
  333.5 5.2 copy.19
  338.7 5.2 copy.21
  343.9 5.2 copy.23
  349.1 5.2 copy.22
  354.3 9.5 %fusion.11 = f32[8,8,512]{2,1,0:T(8,128)} fusion(f32[2048,512]{1,0:T(8,128)} %get-tuple-element.20, f32[2048,512]{1,0:T(8,128)} %get-tuple-element.19, f32[8,8,2048]{2,1,0:T(8,128)S(1)} %get-tuple-element.29, f32[8,8,2048]{2,1,0:T(8,128)S(1)} %get-tuple-element.30), kind=kOutput, calls=%fused_computation.14 | convolution fusion | flops 1615069184 | bytes 9568256 | tf_op jit(solution)/shard_map/dot_general | solution.py:62
  364.0 5.4 copy.25
  369.4 5.2 copy.27
  374.6 5.2 copy.29
  379.8 5.2 copy.28
  385.0 9.5 %fusion.9 = f32[8,8,512]{2,1,0:T(8,128)} fusion(f32[2048,512]{1,0:T(8,128)} %get-tuple-element.20, f32[2048,512]{1,0:T(8,128)} %get-tuple-element.19, f32[8,8,2048]{2,1,0:T(8,128)S(1)} %get-tuple-element.27, f32[8,8,2048]{2,1,0:T(8,128)S(1)} %get-tuple-element.28), kind=kOutput, calls=%fused_computation.13 | convolution fusion | flops 1615069184 | bytes 9568256 | tf_op jit(solution)/shard_map/dot_general | solution.py:62
  394.7 9.5 %fusion.7 = f32[8,8,512]{2,1,0:T(8,128)} fusion(f32[2048,512]{1,0:T(8,128)} %get-tuple-element.20, f32[2048,512]{1,0:T(8,128)} %get-tuple-element.19, f32[8,8,2048]{2,1,0:T(8,128)S(1)} %get-tuple-element.25, f32[8,8,2048]{2,1,0:T(8,128)S(1)} %get-tuple-element.26), kind=kOutput, calls=%fused_computation.12 | convolution fusion | flops 1615069184 | bytes 9568256 | tf_op jit(solution)/shard_map/dot_general | solution.py:62
  404.3 49.5 %reduce-scatter.7.cloned.1.call-done = f32[1,8,512]{2,1,0:T(8,128)} async-done(((f32[8,8,512]{2,1,0:T(8,128)}), f32[1,8,512]{2,1,0:T(8,128)}) %reduce-scatter.7.cloned.1.call-update) | async-done | bytes 16400 | tf_op jit(solution)/shard_map/reduce_scatter | solution.py:87
  453.7 72.4 %reduce-scatter.9.cloned.1.call-done = f32[1,8,512]{2,1,0:T(8,128)} async-done(((f32[8,8,512]{2,1,0:T(8,128)}), f32[1,8,512]{2,1,0:T(8,128)}) %reduce-scatter.9.cloned.1.call-update) | async-done | bytes 16400 | tf_op jit(solution)/shard_map/reduce_scatter | solution.py:87
  526.2 72.3 %reduce-scatter.11.cloned.1.call-done = f32[1,8,512]{2,1,0:T(8,128)} async-done(((f32[8,8,512]{2,1,0:T(8,128)}), f32[1,8,512]{2,1,0:T(8,128)}) %reduce-scatter.11.cloned.1.call-update) | async-done | bytes 16400 | tf_op jit(solution)/shard_map/reduce_scatter | solution.py:87
  (93 shorter events, 12.1 us)
Async XLA Ops:
  6.5 2.8 copy-start.16
  6.5 2.8 copy-start.18
  6.5 397.7 %reduce-scatter.5.cloned.1.call-start = ((), (), s32[]{:S(2)}) async-start(), calls=%async_computation.4 | async-start | bytes 147456 | tf_op jit(solution)/shard_map/reduce_scatter | solution.py:87
  7.7 1.9 copy-start.17
  9.5 18.8 %collective-permute-start = (bf16[8,8,4096]{2,1,0:T(8,128)(2,1)S(1)}, bf16[8,8,4096]{2,1,0:T(8,128)(2,1)S(1)}, u32[]{:S(2)}, u32[]{:S(2)}) collective-permute-start(bf16[8,8,4096]{2,1,0:T(8,128)(2,1)S(1)} %fusion.17), channel_id=1, source_target_pairs={{0,8},{8,0},{16,24},{24,16},{32,40},{40,32},{48,56},{56,48},{64,72... | collective-permute-start | bytes 1572872 | tf_op jit(solution)/shard_map/ppermute | solution.py:12
  28.5 22.2 %collective-permute-start.1 = (bf16[8,8,4096]{2,1,0:T(8,128)(2,1)S(1)}, bf16[8,8,4096]{2,1,0:T(8,128)(2,1)S(1)}, u32[]{:S(2)}, u32[]{:S(2)}) collective-permute-start(bf16[8,8,4096]{2,1,0:T(8,128)(2,1)S(1)} %get-tuple-element.5), channel_id=1, source_target_pairs={{0,16},{8,24},{16,0},{24,8},{32,48},{40,56},{48,32},{56,40},{64,80... | collective-permute-start | bytes 1572872 | tf_op jit(solution)/shard_map/ppermute | solution.py:12
  48.5 14.8 %collective-permute-start.4 = (bf16[8,8,4096]{2,1,0:T(8,128)(2,1)S(1)}, bf16[8,8,4096]{2,1,0:T(8,128)(2,1)S(1)}, u32[]{:S(2)}, u32[]{:S(2)}) collective-permute-start(bf16[8,8,4096]{2,1,0:T(8,128)(2,1)S(1)} %get-tuple-element.8), channel_id=1, source_target_pairs={{0,16},{8,24},{16,0},{24,8},{32,48},{40,56},{48,32},{56,40},{64,80... | collective-permute-start | bytes 1572872 | tf_op jit(solution)/shard_map/ppermute | solution.py:12
  48.6 25.9 %collective-permute-start.7 = (bf16[8,8,4096]{2,1,0:T(8,128)(2,1)S(1)}, bf16[8,8,4096]{2,1,0:T(8,128)(2,1)S(1)}, u32[]{:S(2)}, u32[]{:S(2)}) collective-permute-start(bf16[8,8,4096]{2,1,0:T(8,128)(2,1)S(1)} %get-tuple-element.7), channel_id=1, source_target_pairs={{0,16},{8,24},{16,0},{24,8},{32,48},{40,56},{48,32},{56,40},{64,80... | collective-permute-start | bytes 1572872 | tf_op jit(solution)/shard_map/ppermute | solution.py:12
  50.5 35.2 %collective-permute-start.10 = (bf16[8,8,4096]{2,1,0:T(8,128)(2,1)S(1)}, bf16[8,8,4096]{2,1,0:T(8,128)(2,1)S(1)}, u32[]{:S(2)}, u32[]{:S(2)}) collective-permute-start(bf16[8,8,4096]{2,1,0:T(8,128)(2,1)S(1)} %get-tuple-element.6), channel_id=1, source_target_pairs={{0,16},{8,24},{16,0},{24,8},{32,48},{40,56},{48,32},{56,40},{64,80... | collective-permute-start | bytes 1572872 | tf_op jit(solution)/shard_map/ppermute | solution.py:12
  50.7 48.2 %collective-permute-start.2 = (bf16[8,8,4096]{2,1,0:T(8,128)(2,1)S(1)}, bf16[8,8,4096]{2,1,0:T(8,128)(2,1)S(1)}, u32[]{:S(2)}, u32[]{:S(2)}) collective-permute-start(bf16[8,8,4096]{2,1,0:T(8,128)(2,1)S(1)} %broadcast_select_fusion.13), channel_id=1, source_target_pairs={{0,32},{8,40},{16,48},{24,56},{32,0},{40,8},{48,16},{56,24},{64,96... | collective-permute-start | bytes 1572872 | tf_op jit(solution)/shard_map/ppermute | solution.py:12
  63.3 46.8 %collective-permute-start.5 = (bf16[8,8,4096]{2,1,0:T(8,128)(2,1)S(1)}, bf16[8,8,4096]{2,1,0:T(8,128)(2,1)S(1)}, u32[]{:S(2)}, u32[]{:S(2)}) collective-permute-start(bf16[8,8,4096]{2,1,0:T(8,128)(2,1)S(1)} %broadcast_select_fusion.9), channel_id=1, source_target_pairs={{0,32},{8,40},{16,48},{24,56},{32,0},{40,8},{48,16},{56,24},{64,96... | collective-permute-start | bytes 1572872 | tf_op jit(solution)/shard_map/ppermute | solution.py:12
  74.5 46.8 %collective-permute-start.8 = (bf16[8,8,4096]{2,1,0:T(8,128)(2,1)S(1)}, bf16[8,8,4096]{2,1,0:T(8,128)(2,1)S(1)}, u32[]{:S(2)}, u32[]{:S(2)}) collective-permute-start(bf16[8,8,4096]{2,1,0:T(8,128)(2,1)S(1)} %broadcast_select_fusion.5), channel_id=1, source_target_pairs={{0,32},{8,40},{16,48},{24,56},{32,0},{40,8},{48,16},{56,24},{64,96... | collective-permute-start | bytes 1572872 | tf_op jit(solution)/shard_map/ppermute | solution.py:12
  85.8 46.2 %collective-permute-start.11 = (bf16[8,8,4096]{2,1,0:T(8,128)(2,1)S(1)}, bf16[8,8,4096]{2,1,0:T(8,128)(2,1)S(1)}, u32[]{:S(2)}, u32[]{:S(2)}) collective-permute-start(bf16[8,8,4096]{2,1,0:T(8,128)(2,1)S(1)} %broadcast_select_fusion.1), channel_id=1, source_target_pairs={{0,32},{8,40},{16,48},{24,56},{32,0},{40,8},{48,16},{56,24},{64,96... | collective-permute-start | bytes 1572872 | tf_op jit(solution)/shard_map/ppermute | solution.py:12
  99.0 34.9 %collective-permute-start.3 = (bf16[8,8,4096]{2,1,0:T(8,128)(2,1)S(1)}, bf16[8,8,4096]{2,1,0:T(8,128)(2,1)S(1)}, u32[]{:S(2)}, u32[]{:S(2)}) collective-permute-start(bf16[8,8,4096]{2,1,0:T(8,128)(2,1)S(1)} %broadcast_select_fusion.14), channel_id=1, source_target_pairs={{0,64},{8,72},{16,80},{24,88},{32,96},{40,104},{48,112},{56,120},{... | collective-permute-start | bytes 1572872 | tf_op jit(solution)/shard_map/ppermute | solution.py:12
  110.2 57.6 %collective-permute-start.6 = (bf16[8,8,4096]{2,1,0:T(8,128)(2,1)S(1)}, bf16[8,8,4096]{2,1,0:T(8,128)(2,1)}, u32[]{:S(2)}, u32[]{:S(2)}) collective-permute-start(bf16[8,8,4096]{2,1,0:T(8,128)(2,1)S(1)} %broadcast_select_fusion.10), channel_id=1, source_target_pairs={{0,64},{8,72},{16,80},{24,88},{32,96},{40,104},{48,112},{56,120},{... | collective-permute-start | bytes 1572872 | tf_op jit(solution)/shard_map/ppermute | solution.py:12
  121.5 84.2 %collective-permute-start.9 = (bf16[8,8,4096]{2,1,0:T(8,128)(2,1)S(1)}, bf16[8,8,4096]{2,1,0:T(8,128)(2,1)S(1)}, u32[]{:S(2)}, u32[]{:S(2)}) collective-permute-start(bf16[8,8,4096]{2,1,0:T(8,128)(2,1)S(1)} %broadcast_select_fusion.6), channel_id=1, source_target_pairs={{0,64},{8,72},{16,80},{24,88},{32,96},{40,104},{48,112},{56,120},{... | collective-permute-start | bytes 1572872 | tf_op jit(solution)/shard_map/ppermute | solution.py:12
  132.0 111.8 %collective-permute-start.12 = (bf16[8,8,4096]{2,1,0:T(8,128)(2,1)S(1)}, bf16[8,8,4096]{2,1,0:T(8,128)(2,1)S(1)}, u32[]{:S(2)}, u32[]{:S(2)}) collective-permute-start(bf16[8,8,4096]{2,1,0:T(8,128)(2,1)S(1)} %broadcast_select_fusion.2), channel_id=1, source_target_pairs={{0,64},{8,72},{16,80},{24,88},{32,96},{40,104},{48,112},{56,120},{... | collective-permute-start | bytes 1572872 | tf_op jit(solution)/shard_map/ppermute | solution.py:12
  141.9 9.2 %copy-start.4 = (bf16[8,8,2048]{0,1,2:T(8,128)(2,1)S(1)}, bf16[8,8,2048]{0,1,2:T(8,128)(2,1)}, u32[]{:S(2)}) copy-start(bf16[8,8,2048]{0,1,2:T(8,128)(2,1)} %copy.4) | copy-start | bytes 786436
  141.9 9.2 %copy-start.8 = (bf16[8,8,2048]{1,0,2:T(8,128)(2,1)S(1)}, bf16[8,8,2048]{1,0,2:T(8,128)(2,1)}, u32[]{:S(2)}) copy-start(bf16[8,8,2048]{1,0,2:T(8,128)(2,1)} %copy.5) | copy-start | bytes 786436
  151.1 5.6 copy-start.9
  156.7 5.6 copy-start
  172.2 9.2 %copy-start.1 = (bf16[8,8,2048]{0,1,2:T(8,128)(2,1)S(1)}, bf16[8,8,2048]{0,1,2:T(8,128)(2,1)}, u32[]{:S(2)}) copy-start(bf16[8,8,2048]{0,1,2:T(8,128)(2,1)} %copy.7) | copy-start | bytes 786436
  172.2 9.2 %copy-start.11 = (bf16[8,8,2048]{1,0,2:T(8,128)(2,1)S(1)}, bf16[8,8,2048]{1,0,2:T(8,128)(2,1)}, u32[]{:S(2)}) copy-start(bf16[8,8,2048]{1,0,2:T(8,128)(2,1)} %copy.12) | copy-start | bytes 786436
  190.9 9.2 %copy-start.5 = (bf16[8,8,2048]{0,1,2:T(8,128)(2,1)S(1)}, bf16[8,8,2048]{0,1,2:T(8,128)(2,1)}, u32[]{:S(2)}) copy-start(bf16[8,8,2048]{0,1,2:T(8,128)(2,1)} %copy.4) | copy-start | bytes 786436
  190.9 9.2 %copy-start.12 = (bf16[8,8,2048]{1,0,2:T(8,128)(2,1)S(1)}, bf16[8,8,2048]{1,0,2:T(8,128)(2,1)}, u32[]{:S(2)}) copy-start(bf16[8,8,2048]{1,0,2:T(8,128)(2,1)} %copy.14) | copy-start | bytes 786436
  210.2 9.2 %copy-start.6 = (bf16[8,8,2048]{0,1,2:T(8,128)(2,1)S(1)}, bf16[8,8,2048]{0,1,2:T(8,128)(2,1)}, u32[]{:S(2)}) copy-start(bf16[8,8,2048]{0,1,2:T(8,128)(2,1)} %copy.4) | copy-start | bytes 786436
  210.2 9.2 %copy-start.13 = (bf16[8,8,2048]{1,0,2:T(8,128)(2,1)S(1)}, bf16[8,8,2048]{1,0,2:T(8,128)(2,1)}, u32[]{:S(2)}) copy-start(bf16[8,8,2048]{1,0,2:T(8,128)(2,1)} %copy.20) | copy-start | bytes 786436
  229.0 9.2 %copy-start.2 = (bf16[8,8,2048]{0,1,2:T(8,128)(2,1)S(1)}, bf16[8,8,2048]{0,1,2:T(8,128)(2,1)}, u32[]{:S(2)}) copy-start(bf16[8,8,2048]{0,1,2:T(8,128)(2,1)} %copy.7) | copy-start | bytes 786436
  229.0 9.2 %copy-start.14 = (bf16[8,8,2048]{1,0,2:T(8,128)(2,1)S(1)}, bf16[8,8,2048]{1,0,2:T(8,128)(2,1)}, u32[]{:S(2)}) copy-start(bf16[8,8,2048]{1,0,2:T(8,128)(2,1)} %copy.18) | copy-start | bytes 786436
  248.1 9.2 %copy-start.7 = (bf16[8,8,2048]{0,1,2:T(8,128)(2,1)S(1)}, bf16[8,8,2048]{0,1,2:T(8,128)(2,1)}, u32[]{:S(2)}) copy-start(bf16[8,8,2048]{0,1,2:T(8,128)(2,1)} %copy.4) | copy-start | bytes 786436
  248.1 9.2 %copy-start.15 = (bf16[8,8,2048]{1,0,2:T(8,128)(2,1)S(1)}, bf16[8,8,2048]{1,0,2:T(8,128)(2,1)}, u32[]{:S(2)}) copy-start(bf16[8,8,2048]{1,0,2:T(8,128)(2,1)} %copy.26) | copy-start | bytes 786436
  266.9 9.2 %copy-start.3 = (bf16[8,8,2048]{0,1,2:T(8,128)(2,1)S(1)}, bf16[8,8,2048]{0,1,2:T(8,128)(2,1)}, u32[]{:S(2)}) copy-start(bf16[8,8,2048]{0,1,2:T(8,128)(2,1)} %copy.7) | copy-start | bytes 786436
  266.9 9.2 %copy-start.10 = (bf16[8,8,2048]{1,0,2:T(8,128)(2,1)S(1)}, bf16[8,8,2048]{1,0,2:T(8,128)(2,1)}, u32[]{:S(2)}) copy-start(bf16[8,8,2048]{1,0,2:T(8,128)(2,1)} %copy.24) | copy-start | bytes 786436
  312.5 141.3 %reduce-scatter.7.cloned.1.call-start = ((), (), s32[]{:S(2)}) async-start(), calls=%async_computation.5 | async-start | bytes 147456 | tf_op jit(solution)/shard_map/reduce_scatter | solution.py:87
  363.8 162.3 %reduce-scatter.9.cloned.1.call-start = ((), (), s32[]{:S(2)}) async-start(), calls=%async_computation.6 | async-start | bytes 147456 | tf_op jit(solution)/shard_map/reduce_scatter | solution.py:87
  394.5 203.9 %reduce-scatter.11.cloned.1.call-start = ((), (), s32[]{:S(2)}) async-start(), calls=%async_computation.7 | async-start | bytes 147456 | tf_op jit(solution)/shard_map/reduce_scatter | solution.py:87
Sparse Core Ops, SparseCore 0:
  312.6 68.7 reduce-scatter.4
  384.9 68.7 reduce-scatter.6
  457.3 68.8 reduce-scatter.8
  529.6 68.8 reduce-scatter.10
where the time goes:
time: 613 us; the launch traced here: 607 us
  waiting for transfers between devices  255 us (42%)
  matrix products  153 us (25%)
  local copies, waits for them, and re-layouts  126 us (21%)
  starting transfers between devices  26.2 us (4%)
  between operations  23.7 us (4%)
  other arithmetic  22.4 us (4%)
    reduce_scatter x4, waiting for transfers between devices, per_device(): lax.psum_scatter(term_rows(jnp.int32(0), lax.axis_size('hour') * (chans /...  194 us
    ppermute x13, waiting for transfers between devices, partner_2(): lax.ppermute(value, axis, [(i, i ^ 1 << apart) for i in range(lax.axis_si...  60.9 us
    dot_general x4, matrix products, to_lags(): jnp.dot(flat, weights, precision=lax.Precision.HIGHEST, preferred_element...  38 us
    dot_general x4, matrix products, cross_spectrum(): jnp.einsum('hjf,hif->jif', far_im, own_im, preferred_element_type=f32)  33.1 us
    dot_general x4, matrix products, cross_spectrum(): jnp.einsum('hjf,hif->jif', far_re, own_re, preferred_element_type=f32)  33.1 us
    ppermute x13, starting transfers between devices, partner_2(): lax.ppermute(value, axis, [(i, i ^ 1 << apart) for i in range(lax.axis_si...  26.1 us
    dot_general x4, matrix products, cross_spectrum(): jnp.einsum('hjf,hif->jif', far_re, own_im, preferred_element_type=f32)  25.9 us
    dot_general x4, matrix products, cross_spectrum(): jnp.einsum('hjf,hif->jif', far_im, own_re, preferred_element_type=f32)  22.4 us
  transfers between devices with their start and end apart: 17, of which 10 were waited for; matrix products, arithmetic and copies ran while one was open for 38% of the time, Pallas kernels for 0%

commit v1 on v0

v1 whole, which is shorter than its diff:
```python
import jax
import jax.numpy as jnp
from jax import lax
from jax.sharding import PartitionSpec as P

BAND = 64
LAGS = 512
ROUNDS = 4


def xor_permute(value, axis, mask):
    return lax.ppermute(value, axis, [(i, i ^ mask) for i in range(lax.axis_size(axis))])


def whiten(spectra, quality):
    hours, chans, width = spectra.shape
    n_freq = width // 2
    values = spectra.astype(jnp.float32)
    real_part = values[..., :n_freq]
    imag_part = values[..., n_freq:]
    power_sum = real_part * real_part + imag_part * imag_part
    band_mean = jnp.mean(
        power_sum.reshape(hours, chans, n_freq // BAND, BAND), axis=-1, keepdims=True
    )
    gain_band = lax.rsqrt(band_mean + 1e-06)
    gain_full = jnp.broadcast_to(gain_band, (hours, chans, n_freq // BAND, BAND)).reshape(
        hours, chans, n_freq
    )
    gain_both = jnp.concatenate([gain_full, gain_full], axis=-1)
    scaled = values * gain_both * quality.astype(jnp.float32)[None, :, None]
    return scaled.astype(jnp.bfloat16)


def lag_table(n_freq, total_hours):
    period = 2 * n_freq
    fine_n = 64
    lag_index = jnp.arange(LAGS, dtype=jnp.int32)[None, :] - LAGS // 2

    def angles(freqs):
        phase_int = freqs[:, None] * lag_index % period
        return jnp.pi * phase_int.astype(jnp.float32) / n_freq

    hi = angles(jnp.arange(n_freq // fine_n, dtype=jnp.int32) * fine_n)
    lo = angles(jnp.arange(fine_n, dtype=jnp.int32))
    cos_hi, sin_hi = jnp.cos(hi)[:, None, :], jnp.sin(hi)[:, None, :]
    cos_lo, sin_lo = jnp.cos(lo)[None, :, :], jnp.sin(lo)[None, :, :]
    factor = 1.0 / jnp.sqrt(jnp.float32(total_hours * n_freq))
    cos_t = (cos_hi * cos_lo - sin_hi * sin_lo).reshape(n_freq, LAGS) * factor
    neg_sin_t = (-(sin_hi * cos_lo + cos_hi * sin_lo)).reshape(n_freq, LAGS) * factor
    return cos_t, neg_sin_t


def cross_spectrum(own_block, partner):
    n_freq = own_block.shape[2] // 2
    a = own_block.astype(jnp.float32)
    b = partner.astype(jnp.float32)
    a_re = a[:, None, :, :n_freq]
    a_im = a[:, None, :, n_freq:]
    b_re = b[:, :, None, :n_freq]
    b_im = b[:, :, None, n_freq:]
    cross_re = jnp.sum(b_re * a_re + b_im * a_im, axis=0)
    cross_im = jnp.sum(b_re * a_im - b_im * a_re, axis=0)
    return cross_re, cross_im


def per_device(spectra, quality, plan):
    hours, chans, width = spectra.shape
    n_freq = width // 2
    n_chan = lax.axis_size("chan")
    n_hour = lax.axis_size("hour")
    own_block = whiten(spectra, quality)
    cos_t, neg_sin_t = lag_table(n_freq, hours * n_hour)

    others = (plan != 1) & (plan != n_chan - 1)
    first = jnp.argmax(others).astype(jnp.int32)
    last = (ROUNDS - 1 - jnp.argmax(others[::-1])).astype(jnp.int32)
    branches = [
        (lambda v, m=m: xor_permute(v, "chan", m)) for m in range(1, n_chan)
    ]
    partners = [
        xor_permute(own_block, "chan", 1),
        xor_permute(own_block, "chan", n_chan - 1),
        lax.switch(plan[first] - 1, branches, own_block),
        lax.switch(plan[last] - 1, branches, own_block),
    ]
    re_parts, im_parts = [], []
    for partner in partners:
        cross_re, cross_im = cross_spectrum(own_block, partner)
        re_parts.append(cross_re)
        im_parts.append(cross_im)
    cross_re = jnp.stack(re_parts, axis=1).reshape(-1, n_freq)
    cross_im = jnp.stack(im_parts, axis=1).reshape(-1, n_freq)
    hp = lax.Precision.HIGHEST
    lagged = jnp.dot(cross_re, cos_t, precision=hp, preferred_element_type=jnp.float32)
    lagged = lagged + jnp.dot(
        cross_im, neg_sin_t, precision=hp, preferred_element_type=jnp.float32
    )
    lagged = lagged.reshape(chans, ROUNDS * chans, LAGS)

    me = lax.axis_index("hour")
    total = lax.dynamic_index_in_dim(lagged, me, axis=0, keepdims=False)
    for dist in range(1, n_hour):
        piece = lax.dynamic_index_in_dim(lagged, me ^ dist, axis=0, keepdims=False)
        total = total + xor_permute(piece, "hour", dist)
    total = total.reshape(ROUNDS, chans, LAGS)

    slot = jnp.where(
        plan == 1,
        0,
        jnp.where(
            plan == n_chan - 1,
            1,
            jnp.where(jnp.arange(ROUNDS, dtype=jnp.int32) == first, 2, 3),
        ),
    ).astype(jnp.int32)
    result = jnp.take(total, slot, axis=0)
    return result[:, None]


def solution(mesh):
    return jax.shard_map(
        per_device,
        mesh=mesh,
        in_specs=(P("hour", "chan", None), P("chan"), P()),
        out_specs=P(None, "hour", "chan", None),
        check_vma=False,
    )
```

time: 613 us -> 97.4 us (0.16); the launches traced: 607 us -> 98.8 us
  waiting for transfers between devices: 255 us -> 39.2 us
  matrix products: 153 us -> 7.4 us
  local copies, waits for them, and re-layouts: 126 us -> 9.26 us
  between operations: 23.7 us -> 4.71 us
    reduce_scatter x4 -> x0, waiting for transfers between devices: 194 us -> none  [per_device(): lax.psum_scatter(term_rows(jnp.int32(0), lax.axis_size('hour') * (chans /...]
    dot_general x20 -> x2, matrix products: 153 us -> 7.4 us  [the longest x1 3.72 us: per_device(): jnp.dot(cross_im, neg_sin_t, precision=hp, preferred_element_type=jnp.flo...]
    dot_general x16 -> x0, local copies, waits for them, and re-layouts: 83.7 us -> none  [the longest x4 21.2 us: cross_spectrum(): jnp.einsum('hjf,hif->jif', far_im, own_im, preferred_element_type=f32)]
    slice x16 -> x4, local copies, waits for them, and re-layouts: 41.6 us -> 3.71 us  [the longest x3 2.59 us: cross_spectrum(): b_re = b[:, :, None, :n_freq]]
    ppermute x13 -> x11, waiting for transfers between devices: 60.9 us -> 39.2 us  [xor_permute(): lax.ppermute(value, axis, [(i, i ^ mask) for i in range(lax.axis_size(axi...]
    cos x1 -> x2, other arithmetic: 17.9 us -> 0.86 us  [the longest x1 0.53 us: lag_table(): cos_lo, sin_lo = (jnp.cos(lo)[None, :, :], jnp.sin(lo)[None, :, :])]
    ppermute x13 -> x11, starting transfers between devices: 26.1 us -> 21.3 us  [xor_permute(): lax.ppermute(value, axis, [(i, i ^ mask) for i in range(lax.axis_size(axi...]
  transfers between devices with their start and end apart: 17 -> 11, of which waited for: 10 -> 4; matrix products, arithmetic and copies ran while one was open for 38% -> 12% of each run, Pallas kernels for 0% -> 0%
where the time goes in v1:
time: 97.4 us; the launch traced here: 98.8 us
  waiting for transfers between devices  39.2 us (40%)
  starting transfers between devices  21.3 us (22%)
  other arithmetic  16.8 us (17%)
  local copies, waits for them, and re-layouts  9.26 us (10%)
  matrix products  7.4 us (8%)
  between operations  4.71 us (5%)
    ppermute x11, waiting for transfers between devices, xor_permute(): lax.ppermute(value, axis, [(i, i ^ mask) for i in range(lax.axis_size(axi...  39.2 us
    ppermute x11, starting transfers between devices, xor_permute(): lax.ppermute(value, axis, [(i, i ^ mask) for i in range(lax.axis_size(axi...  21.3 us
    reduce_sum x1, other arithmetic, cross_spectrum(): cross_im = jnp.sum(b_re * a_im - b_im * a_re, axis=0)  5.75 us
    mul x1, other arithmetic, lag_table(): (-(sin_hi * cos_lo + cos_hi * sin_lo)).reshape(n_freq, LAGS) * factor  4.5 us
    dot_general x1, matrix products, per_device(): jnp.dot(cross_im, neg_sin_t, precision=hp, preferred_element_type=jnp.flo...  3.72 us
    dot_general x1, matrix products, per_device(): jnp.dot(cross_re, cos_t, precision=hp, preferred_element_type=jnp.float32)  3.68 us
    unnamed x14, local copies, waits for them, and re-layouts  2.85 us
    slice x3, local copies, waits for them, and re-layouts, cross_spectrum(): b_re = b[:, :, None, :n_freq]  2.59 us
  transfers between devices with their start and end apart: 11, of which 4 were waited for; matrix products, arithmetic and copies ran while one was open for 12% of the time, Pallas kernels for 0%

profile of v1, /device:TPU:0, one launch (start us, length us, event | category | flops | bytes accessed | tf_op | source)
XLA Modules:
  0.0 98.8 jit_solution(17159188914342714165)
XLA Ops:
  0.0 0.0 copy-start.2
  0.0 0.0 copy-start.6
  0.0 1.2 %convert_element_type.141 = f32[8,8,4096]{2,1,0:T(8,128)S(1)} convert(bf16[8,8,4096]{2,1,0:T(8,128)(2,1)} %param.33) | non-fusion elementwise | flops 262144 | bytes 1572864 | tf_op jit(solution)/shard_map/convert_element_type | solution.py:18
  1.2 0.1 fusion.2
  1.3 0.0 copy-start.5
  1.3 0.4 reshape.223
  1.7 0.3 reduce_sum.81
  2.1 0.3 broadcast_in_dim.25
  2.4 0.4 reshape.224
  2.8 0.0 copy-done.6
  2.8 0.0 copy-done.2
  2.8 1.0 %fusion.1 = bf16[8,8,4096]{2,1,0:T(8,128)(2,1)} fusion(f32[8,8,2048]{2,1,0:T(8,128)S(1)} %reshape.224, f32[8]{0:T(128)S(1)} %convert_element_type.142, bf16[8,8,4096]{2,1,0:T(8,128)(2,1)S(1)} %copy-done.2), kind=kLoop, calls=%fused_computation.16 | loop fusion | flops 1310720 | bytes 1572896 | tf_op jit(solution)/shard_map/convert_element_type | solution.py:31
  3.8 0.0 collective-permute-start.30
  3.8 5.2 %collective-permute-start.31 = (bf16[8,8,4096]{2,1,0:T(8,128)(2,1)}, bf16[8,8,4096]{2,1,0:T(8,128)(2,1)S(1)}, u32[]{:S(2)}, u32[]{:S(2)}) collective-permute-start(bf16[8,8,4096]{2,1,0:T(8,128)(2,1)} %fusion.1), channel_id=1, source_target_pairs={{0,120},{8,112},{16,104},{24,96},{32,88},{40,80},{48,72},{56,64},{... | collective-permute-start | bytes 1572872 | tf_op jit(solution)/shard_map/ppermute | solution.py:12
  9.0 1.1 %fusion.27 = (f32[8,8,2048]{2,1,0:T(8,128)S(1)}, f32[8,8,2048]{2,1,0:T(8,128)S(1)}) fusion(bf16[8,8,4096]{2,1,0:T(8,128)(2,1)} %fusion.1), kind=kLoop, calls=%fused_computation.72 | loop fusion | bytes 2097152 | tf_op jit(solution)/shard_map/slice | solution.py:57
  10.2 0.0 copy-done.5
  10.2 0.7 iota_reduce_fusion.1
  10.9 0.6 broadcast_compare_fusion
  11.5 0.1 rev.3
  11.6 0.7 iota_reduce_fusion
  15.5 0.6 fusion.28
  16.7 15.7 %conditional.2 = (bf16[8,8,4096]{2,1,0:T(8,128)(2,1)}) conditional(s32[]{:T(128)} %bitcast.2, bf16[8,8,4096]{2,1,0:T(8,128)(2,1)} %fusion.1, bf16[8,8,4096]{2,1,0:T(8,128)(2,1)} %fusion.1, bf16[8,8,4096]{2,1,0:T(8,128)(2,1)} %fusion.1, bf16[8,8,4096]{2,1,0:T(8,128)(2,1)} %fusion.1, ...), branch_computations={%region_4.5_spmd, %region_5.6_spmd, %region_6.7_spmd, %region_7.8_... | conditional | bytes 2097200 | solution.py:83
  16.8 0.1 collective-permute-start.8
  16.9 15.6 %collective-permute-done.8 = bf16[8,8,4096]{2,1,0:T(8,128)(2,1)} collective-permute-done((bf16[8,8,4096]{2,1,0:T(8,128)(2,1)}, bf16[8,8,4096]{2,1,0:T(8,128)(2,1)}, u32[]{:S(2)}, u32[]{:S(2)}) %collective-permute-start.8) | collective-permute-done | bytes 524320 | tf_op jit(solution)/shard_map/cond/branch_8_fun/ppermute | solution.py:12
  33.1 17.1 %conditional.3 = (bf16[8,8,4096]{2,1,0:T(8,128)(2,1)}) conditional(s32[]{:T(128)} %bitcast.4, bf16[8,8,4096]{2,1,0:T(8,128)(2,1)} %fusion.1, bf16[8,8,4096]{2,1,0:T(8,128)(2,1)} %fusion.1, bf16[8,8,4096]{2,1,0:T(8,128)(2,1)} %fusion.1, bf16[8,8,4096]{2,1,0:T(8,128)(2,1)} %fusion.1, ...), branch_computations={%region_21.22_spmd, %region_22.23_spmd, %region_23.24_spmd, %regio... | conditional | bytes 2097200 | solution.py:84
  33.2 1.0 %collective-permute-start.26 = (bf16[8,8,4096]{2,1,0:T(8,128)(2,1)}, bf16[8,8,4096]{2,1,0:T(8,128)(2,1)}, u32[]{:S(2)}, u32[]{:S(2)}) collective-permute-start(bf16[8,8,4096]{2,1,0:T(8,128)(2,1)} %param.26), channel_id=1, source_target_pairs={{0,96},{8,104},{16,112},{24,120},{32,64},{40,72},{48,80},{56,88},{... | collective-permute-start | bytes 1572872 | tf_op jit(solution)/shard_map/cond/branch_11_fun/ppermute | solution.py:12
  34.2 16.1 %collective-permute-done.26 = bf16[8,8,4096]{2,1,0:T(8,128)(2,1)} collective-permute-done((bf16[8,8,4096]{2,1,0:T(8,128)(2,1)}, bf16[8,8,4096]{2,1,0:T(8,128)(2,1)}, u32[]{:S(2)}, u32[]{:S(2)}) %collective-permute-start.26) | collective-permute-done | bytes 524320 | tf_op jit(solution)/shard_map/cond/branch_11_fun/ppermute | solution.py:12
  50.3 0.5 fusion.20
  50.8 2.4 %fusion.23 = (f32[8,8,2048]{2,1,0:T(8,128)S(1)}, f32[8,8,2048]{2,1,0:T(8,128)S(1)}, f32[8,8,2048]{2,1,0:T(8,128)}, f32[8,8,2048]{2,1,0:T(8,128)}) fusion(bf16[8,8,4096]{2,1,0:T(8,128)(2,1)} %get-tuple-element.116, bf16[8,8,4096]{2,1,0:T(8,128)(2,1)} %get-tuple-element.115), kind=kLoop, calls=%fused_computation.68 | loop fusion | bytes 4194304 | tf_op jit(solution)/shard_map/slice | solution.py:59
  53.2 0.3 fusion.22
  53.5 4.5 %negate_multiply_fusion = (f32[32,64,512]{2,1,0:T(8,128)}, f32[32,64,512]{2,1,0:T(8,128)}) fusion(f32[64,512]{1,0:T(8,128)S(1)} %get-tuple-element.109, f32[32,512]{1,0:T(8,128)S(1)} %get-tuple-element.107, f32[64,512]{1,0:T(8,128)S(1)} %get-tuple-element.108, f32[32,512]{1,0:T(8,128)S(1)} %get-tuple-element.106), kind=kLoop, calls=%fused_computation.1 | loop fusion | flops 9437184 | bytes 8781824 | tf_op jit(solution)/shard_map/mul | solution.py:49
  58.0 0.0 collective-permute-done.30
  58.0 0.1 fusion.26
  58.1 0.0 collective-permute-done.31
  58.1 0.1 fusion.25
  58.2 0.8 copy-done.3
  59.1 0.2 copy-done.4
  59.2 5.8 %subtract_reduce_fusion.3 = (f32[8,8,2048]{2,1,0:T(8,128)S(1)}, f32[8,8,2048]{2,1,0:T(8,128)S(1)}, f32[8,8,2048]{2,1,0:T(8,128)S(1)}, f32[8,8,2048]{2,1,0:T(8,12...) fusion(f32[8,8,2048]{2,1,0:T(8,128)S(1)} %get-tuple-element.103, ...), kind=kLoop, calls=%fused_computation.5 | loop fusion | flops 32505856 | bytes 9437184 | tf_op jit(solution)/shard_map/reduce_sum | solution.py:62
  65.0 0.1 pad_maximum_fusion.1
  65.1 0.1 copy.5
  65.3 0.0 copy-start.1
  65.3 0.2 pad_maximum_fusion
  65.5 0.1 copy.4
  65.6 0.0 copy-start
  65.6 1.8 %copy-done.1 = f32[32,64,512]{2,1,0:T(8,128)S(1)} copy-done((f32[32,64,512]{2,1,0:T(8,128)S(1)}, f32[32,64,512]{2,1,0:T(8,128)}, u32[]{:S(2)}) %copy-start.1) | copy-done | bytes 4194328
  67.5 3.7 %fusion.29 = f32[256,512]{1,0:T(8,128)S(1)} fusion(f32[256,2048]{1,0:T(8,128)S(1)} %bitcast.58, f32[2048,512]{1,0:T(8,128)S(1)} %bitcast.56), kind=kOutput, calls=%fused_computation.74 | convolution fusion | flops 3221225472 | bytes 6815744 | tf_op jit(solution)/shard_map/dot_general | solution.py:94
  71.2 0.0 copy-done
  71.2 3.7 %convolution_add_fusion = f32[256,512]{1,0:T(8,128)S(1)} fusion(f32[256,512]{1,0:T(8,128)S(1)} %fusion.29, f32[256,2048]{1,0:T(8,128)S(1)} %bitcast.57, f32[2048,512]{1,0:T(8,128)S(1)} %bitcast.55), kind=kOutput, calls=%fused_computation.13 | convolution fusion | flops 3221356544 | bytes 7340032 | tf_op jit(solution)/shard_map/dot_general | solution.py:95
  75.0 1.6 %collective-permute-start.32 = (f32[32,512]{1,0:T(8,128)S(1)}, f32[32,512]{1,0:T(8,128)S(1)}, u32[]{:S(2)}, u32[]{:S(2)}) collective-permute-start(f32[32,512]{1,0:T(8,128)S(1)} %get-tuple-element.87), channel_id=1, source_target_pairs={{0,1},{1,0},{2,3},{3,2},{4,5},{5,4},{6,7},{7,6},{8,9},{9,8},{10,11... | collective-permute-start | bytes 196616 | tf_op jit(solution)/shard_map/ppermute | solution.py:12
  76.5 2.7 %collective-permute-start.33 = (f32[32,512]{1,0:T(8,128)S(1)}, f32[32,512]{1,0:T(8,128)S(1)}, u32[]{:S(2)}, u32[]{:S(2)}) collective-permute-start(f32[32,512]{1,0:T(8,128)S(1)} %get-tuple-element.93), channel_id=1, source_target_pairs={{0,2},{1,3},{2,0},{3,1},{4,6},{5,7},{6,4},{7,5},{8,10},{9,11},{10,... | collective-permute-start | bytes 196616 | tf_op jit(solution)/shard_map/ppermute | solution.py:12
  79.3 0.5 collective-permute-start.34
  79.7 3.2 %collective-permute-start.35 = (f32[32,512]{1,0:T(8,128)S(1)}, f32[32,512]{1,0:T(8,128)S(1)}, u32[]{:S(2)}, u32[]{:S(2)}) collective-permute-start(f32[32,512]{1,0:T(8,128)S(1)} %get-tuple-element.91), channel_id=1, source_target_pairs={{0,4},{1,5},{2,6},{3,7},{4,0},{5,1},{6,2},{7,3},{8,12},{9,13},{10,... | collective-permute-start | bytes 196616 | tf_op jit(solution)/shard_map/ppermute | solution.py:12
  82.9 0.1 collective-permute-start.36
  83.0 0.0 collective-permute-done.32
  83.0 6.6 %collective-permute-start.37 = (f32[32,512]{1,0:T(8,128)S(1)}, f32[32,512]{1,0:T(8,128)S(1)}, u32[]{:S(2)}, u32[]{:S(2)}) collective-permute-start(f32[32,512]{1,0:T(8,128)S(1)} %get-tuple-element.89), channel_id=1, source_target_pairs={{0,6},{1,7},{2,4},{3,5},{4,2},{5,3},{6,0},{7,1},{8,14},{9,15},{10,... | collective-permute-start | bytes 196616 | tf_op jit(solution)/shard_map/ppermute | solution.py:12
  89.6 0.0 collective-permute-done.33
  89.6 0.2 collective-permute-start.38
  89.8 0.0 collective-permute-done.34
  89.8 0.0 collective-permute-done.35
  89.8 0.0 collective-permute-done.36
  89.8 2.7 %collective-permute-done.37 = f32[32,512]{1,0:T(8,128)S(1)} collective-permute-done((f32[32,512]{1,0:T(8,128)S(1)}, f32[32,512]{1,0:T(8,128)S(1)}, u32[]{:S(2)}, u32[]{:S(2)}) %collective-permute-start.37) | collective-permute-done | bytes 65568 | tf_op jit(solution)/shard_map/ppermute | solution.py:12
  92.5 4.9 %collective-permute-done.38 = f32[32,512]{1,0:T(8,128)S(1)} collective-permute-done((f32[32,512]{1,0:T(8,128)S(1)}, f32[32,512]{1,0:T(8,128)S(1)}, u32[]{:S(2)}, u32[]{:S(2)}) %collective-permute-start.38) | collective-permute-done | bytes 65568 | tf_op jit(solution)/shard_map/ppermute | solution.py:12
  97.5 0.6 gather_fusion
  98.1 0.7 bitcast_select_fusion
  (9 shorter events, 0.1 us)
Async XLA Ops:
  0.0 2.8 %copy-start.2 = (bf16[8,8,4096]{2,1,0:T(8,128)(2,1)S(1)}, bf16[8,8,4096]{2,1,0:T(8,128)(2,1)}, u32[]{:S(2)}) copy-start(bf16[8,8,4096]{2,1,0:T(8,128)(2,1)} %param.33) | copy-start | bytes 1572868
  0.0 2.8 %copy-start.6 = (s32[8]{0:T(128)S(1)}, s32[8]{0:T(128)}, u32[]{:S(2)}) copy-start(s32[8]{0:T(128)} %param.34) | copy-start | bytes 100
  1.3 8.9 %copy-start.5 = (s32[4]{0:T(128)S(1)}, s32[4]{0:T(128)}, u32[]{:S(2)}) copy-start(s32[4]{0:T(128)} %param.35) | copy-start | bytes 52
  3.8 54.3 %collective-permute-start.30 = (bf16[8,8,4096]{2,1,0:T(8,128)(2,1)}, bf16[8,8,4096]{2,1,0:T(8,128)(2,1)S(1)}, u32[]{:S(2)}, u32[]{:S(2)}) collective-permute-start(bf16[8,8,4096]{2,1,0:T(8,128)(2,1)} %fusion.1), channel_id=1, source_target_pairs={{0,8},{8,0},{16,24},{24,16},{32,40},{40,32},{48,56},{56,48},{64,72... | collective-permute-start | bytes 1572872 | tf_op jit(solution)/shard_map/ppermute | solution.py:12
  3.8 54.4 %collective-permute-start.31 = (bf16[8,8,4096]{2,1,0:T(8,128)(2,1)}, bf16[8,8,4096]{2,1,0:T(8,128)(2,1)S(1)}, u32[]{:S(2)}, u32[]{:S(2)}) collective-permute-start(bf16[8,8,4096]{2,1,0:T(8,128)(2,1)} %fusion.1), channel_id=1, source_target_pairs={{0,120},{8,112},{16,104},{24,96},{32,88},{40,80},{48,72},{56,64},{... | collective-permute-start | bytes 1572872 | tf_op jit(solution)/shard_map/ppermute | solution.py:12
  16.8 15.7 %collective-permute-start.8 = (bf16[8,8,4096]{2,1,0:T(8,128)(2,1)}, bf16[8,8,4096]{2,1,0:T(8,128)(2,1)}, u32[]{:S(2)}, u32[]{:S(2)}) collective-permute-start(bf16[8,8,4096]{2,1,0:T(8,128)(2,1)} %param.8), channel_id=1, source_target_pairs={{0,72},{8,64},{16,88},{24,80},{32,104},{40,96},{48,120},{56,112},{... | collective-permute-start | bytes 1572872 | tf_op jit(solution)/shard_map/cond/branch_8_fun/ppermute | solution.py:12
  33.2 17.1 %collective-permute-start.26 = (bf16[8,8,4096]{2,1,0:T(8,128)(2,1)}, bf16[8,8,4096]{2,1,0:T(8,128)(2,1)}, u32[]{:S(2)}, u32[]{:S(2)}) collective-permute-start(bf16[8,8,4096]{2,1,0:T(8,128)(2,1)} %param.26), channel_id=1, source_target_pairs={{0,96},{8,104},{16,112},{24,120},{32,64},{40,72},{48,80},{56,88},{... | collective-permute-start | bytes 1572872 | tf_op jit(solution)/shard_map/cond/branch_11_fun/ppermute | solution.py:12
  58.0 1.0 %copy-start.3 = (f32[8,8,2048]{2,1,0:T(8,128)S(1)}, f32[8,8,2048]{2,1,0:T(8,128)}, u32[]{:S(2)}) copy-start(f32[8,8,2048]{2,1,0:T(8,128)} %get-tuple-element.113) | copy-start | bytes 1572868
  58.0 1.2 %copy-start.4 = (f32[8,8,2048]{2,1,0:T(8,128)S(1)}, f32[8,8,2048]{2,1,0:T(8,128)}, u32[]{:S(2)}) copy-start(f32[8,8,2048]{2,1,0:T(8,128)} %get-tuple-element.114) | copy-start | bytes 1572868
  65.3 2.2 %copy-start.1 = (f32[32,64,512]{2,1,0:T(8,128)S(1)}, f32[32,64,512]{2,1,0:T(8,128)}, u32[]{:S(2)}) copy-start(f32[32,64,512]{2,1,0:T(8,128)} %get-tuple-element.105) | copy-start | bytes 12582916
  65.6 5.5 %copy-start = (f32[32,64,512]{2,1,0:T(8,128)S(1)}, f32[32,64,512]{2,1,0:T(8,128)}, u32[]{:S(2)}) copy-start(f32[32,64,512]{2,1,0:T(8,128)} %get-tuple-element.104) | copy-start | bytes 12582916
  75.0 8.0 %collective-permute-start.32 = (f32[32,512]{1,0:T(8,128)S(1)}, f32[32,512]{1,0:T(8,128)S(1)}, u32[]{:S(2)}, u32[]{:S(2)}) collective-permute-start(f32[32,512]{1,0:T(8,128)S(1)} %get-tuple-element.87), channel_id=1, source_target_pairs={{0,1},{1,0},{2,3},{3,2},{4,5},{5,4},{6,7},{7,6},{8,9},{9,8},{10,11... | collective-permute-start | bytes 196616 | tf_op jit(solution)/shard_map/ppermute | solution.py:12
  76.5 13.0 %collective-permute-start.33 = (f32[32,512]{1,0:T(8,128)S(1)}, f32[32,512]{1,0:T(8,128)S(1)}, u32[]{:S(2)}, u32[]{:S(2)}) collective-permute-start(f32[32,512]{1,0:T(8,128)S(1)} %get-tuple-element.93), channel_id=1, source_target_pairs={{0,2},{1,3},{2,0},{3,1},{4,6},{5,7},{6,4},{7,5},{8,10},{9,11},{10,... | collective-permute-start | bytes 196616 | tf_op jit(solution)/shard_map/ppermute | solution.py:12
  79.3 10.6 %collective-permute-start.34 = (f32[32,512]{1,0:T(8,128)S(1)}, f32[32,512]{1,0:T(8,128)S(1)}, u32[]{:S(2)}, u32[]{:S(2)}) collective-permute-start(f32[32,512]{1,0:T(8,128)S(1)} %get-tuple-element.92), channel_id=1, source_target_pairs={{0,3},{1,2},{2,1},{3,0},{4,7},{5,6},{6,5},{7,4},{8,11},{9,10},{10,... | collective-permute-start | bytes 196616 | tf_op jit(solution)/shard_map/ppermute | solution.py:12
  79.7 10.1 %collective-permute-start.35 = (f32[32,512]{1,0:T(8,128)S(1)}, f32[32,512]{1,0:T(8,128)S(1)}, u32[]{:S(2)}, u32[]{:S(2)}) collective-permute-start(f32[32,512]{1,0:T(8,128)S(1)} %get-tuple-element.91), channel_id=1, source_target_pairs={{0,4},{1,5},{2,6},{3,7},{4,0},{5,1},{6,2},{7,3},{8,12},{9,13},{10,... | collective-permute-start | bytes 196616 | tf_op jit(solution)/shard_map/ppermute | solution.py:12
  82.9 6.9 %collective-permute-start.36 = (f32[32,512]{1,0:T(8,128)S(1)}, f32[32,512]{1,0:T(8,128)S(1)}, u32[]{:S(2)}, u32[]{:S(2)}) collective-permute-start(f32[32,512]{1,0:T(8,128)S(1)} %get-tuple-element.90), channel_id=1, source_target_pairs={{0,5},{1,4},{2,7},{3,6},{4,1},{5,0},{6,3},{7,2},{8,13},{9,12},{10,... | collective-permute-start | bytes 196616 | tf_op jit(solution)/shard_map/ppermute | solution.py:12
  83.0 9.5 %collective-permute-start.37 = (f32[32,512]{1,0:T(8,128)S(1)}, f32[32,512]{1,0:T(8,128)S(1)}, u32[]{:S(2)}, u32[]{:S(2)}) collective-permute-start(f32[32,512]{1,0:T(8,128)S(1)} %get-tuple-element.89), channel_id=1, source_target_pairs={{0,6},{1,7},{2,4},{3,5},{4,2},{5,3},{6,0},{7,1},{8,14},{9,15},{10,... | collective-permute-start | bytes 196616 | tf_op jit(solution)/shard_map/ppermute | solution.py:12
  89.6 7.9 %collective-permute-start.38 = (f32[32,512]{1,0:T(8,128)S(1)}, f32[32,512]{1,0:T(8,128)S(1)}, u32[]{:S(2)}, u32[]{:S(2)}) collective-permute-start(f32[32,512]{1,0:T(8,128)S(1)} %get-tuple-element.88), channel_id=1, source_target_pairs={{0,7},{1,6},{2,5},{3,4},{4,3},{5,2},{6,1},{7,0},{8,15},{9,14},{10,... | collective-permute-start | bytes 196616 | tf_op jit(solution)/shard_map/ppermute | solution.py:12

commit v2 on v1

--- a/solution.py
+++ b/solution.py
@@ -97,12 +97,8 @@
     )
     lagged = lagged.reshape(chans, ROUNDS * chans, LAGS)
 
-    me = lax.axis_index("hour")
-    total = lax.dynamic_index_in_dim(lagged, me, axis=0, keepdims=False)
-    for dist in range(1, n_hour):
-        piece = lax.dynamic_index_in_dim(lagged, me ^ dist, axis=0, keepdims=False)
-        total = total + xor_permute(piece, "hour", dist)
-    total = total.reshape(ROUNDS, chans, LAGS)
+    gathered = lax.all_to_all(lagged, "hour", 0, 0, tiled=True)
+    total = jnp.sum(gathered, axis=0).reshape(ROUNDS, chans, LAGS)
 
     slot = jnp.where(
         plan == 1,

time: 97.4 us -> 86.1 us (0.88); the launches traced: 98.8 us -> 86 us
  starting transfers between devices: 21.3 us -> 12.5 us
  local copies, waits for them, and re-layouts: 9.26 us -> 5.46 us
  other arithmetic: 16.8 us -> 13.5 us
  waiting for transfers between devices: 39.2 us -> 41.5 us
    ppermute x11 -> x4, starting transfers between devices: 21.3 us -> 5.63 us  [xor_permute(): lax.ppermute(value, axis, [(i, i ^ mask) for i in range(lax.axis_size(axi...]
    all_to_all x0 -> x1, waiting for transfers between devices: none -> 11 us  [per_device(): gathered = lax.all_to_all(lagged, 'hour', 0, 0, tiled=True)]
    ppermute x11 -> x4, waiting for transfers between devices: 39.2 us -> 30.5 us  [xor_permute(): lax.ppermute(value, axis, [(i, i ^ mask) for i in range(lax.axis_size(axi...]
    all_to_all x0 -> x1, starting transfers between devices: none -> 6.84 us  [per_device(): gathered = lax.all_to_all(lagged, 'hour', 0, 0, tiled=True)]
    mul x1, other arithmetic: 4.5 us -> 1.17 us  [lag_table(): (-(sin_hi * cos_lo + cos_hi * sin_lo)).reshape(n_freq, LAGS) * factor]
    unnamed x14 -> x6, local copies, waits for them, and re-layouts: 2.85 us -> 0.01 us
    slice x3, local copies, waits for them, and re-layouts: 2.59 us -> 1.61 us  [cross_spectrum(): b_re = b[:, :, None, :n_freq]]
  transfers between devices with their start and end apart: 11 -> 5, of which waited for: 4 -> 3; matrix products, arithmetic and copies ran while one was open for 12% -> 9% of each run, Pallas kernels for 0% -> 0%
where the time goes in v2:
time: 86.1 us; the launch traced here: 86 us
  waiting for transfers between devices  41.5 us (48%)
  other arithmetic  13.5 us (16%)
  starting transfers between devices  12.5 us (15%)
  matrix products  8.19 us (10%)
  local copies, waits for them, and re-layouts  5.46 us (6%)
  between operations  4.79 us (6%)
    ppermute x4, waiting for transfers between devices, xor_permute(): lax.ppermute(value, axis, [(i, i ^ mask) for i in range(lax.axis_size(axi...  30.5 us
    all_to_all x1, waiting for transfers between devices, per_device(): gathered = lax.all_to_all(lagged, 'hour', 0, 0, tiled=True)  11 us
    all_to_all x1, starting transfers between devices, per_device(): gathered = lax.all_to_all(lagged, 'hour', 0, 0, tiled=True)  6.84 us
    reduce_sum x1, other arithmetic, cross_spectrum(): cross_im = jnp.sum(b_re * a_im - b_im * a_re, axis=0)  5.78 us
    ppermute x4, starting transfers between devices, xor_permute(): lax.ppermute(value, axis, [(i, i ^ mask) for i in range(lax.axis_size(axi...  5.63 us
    dot_general x1, matrix products, per_device(): jnp.dot(cross_im, neg_sin_t, precision=hp, preferred_element_type=jnp.flo...  4.51 us
    dot_general x1, matrix products, per_device(): jnp.dot(cross_re, cos_t, precision=hp, preferred_element_type=jnp.float32)  3.69 us
  transfers between devices with their start and end apart: 5, of which 3 were waited for; matrix products, arithmetic and copies ran while one was open for 9% of the time, Pallas kernels for 0%

profile of v2, /device:TPU:0, one launch (start us, length us, event | category | flops | bytes accessed | tf_op | source)
XLA Modules:
  0.0 86.0 jit_solution(10943683663323959249)
XLA Ops:
  0.0 0.0 copy-start
  0.0 0.0 copy-start.2
  0.0 1.2 %convert_element_type.141 = f32[8,8,4096]{2,1,0:T(8,128)S(1)} convert(bf16[8,8,4096]{2,1,0:T(8,128)(2,1)} %param.33) | non-fusion elementwise | flops 262144 | bytes 1572864 | tf_op jit(solution)/shard_map/convert_element_type | solution.py:18
  1.2 0.1 fusion.2
  1.3 0.0 copy-start.1
  1.3 0.4 reshape.223
  1.7 0.3 reduce_sum.90
  2.1 0.3 broadcast_in_dim.25
  2.4 0.4 reshape.224
  2.8 0.0 copy-done.2
  2.8 0.0 copy-done
  2.8 0.9 %fusion.1 = bf16[8,8,4096]{2,1,0:T(8,128)(2,1)} fusion(f32[8,8,2048]{2,1,0:T(8,128)S(1)} %reshape.224, f32[8]{0:T(128)S(1)} %convert_element_type.142, bf16[8,8,4096]{2,1,0:T(8,128)(2,1)S(1)} %copy-done), kind=kLoop, calls=%fused_computation.16 | loop fusion | flops 1310720 | bytes 1572896 | tf_op jit(solution)/shard_map/convert_element_type | solution.py:31
  3.7 4.6 %collective-permute-start.31 = (bf16[8,8,4096]{2,1,0:T(8,128)(2,1)}, bf16[8,8,4096]{2,1,0:T(8,128)(2,1)S(1)}, u32[]{:S(2)}, u32[]{:S(2)}) collective-permute-start(bf16[8,8,4096]{2,1,0:T(8,128)(2,1)} %fusion.1), channel_id=1, source_target_pairs={{0,120},{8,112},{16,104},{24,96},{32,88},{40,80},{48,72},{56,64},{... | collective-permute-start | bytes 1572872 | tf_op jit(solution)/shard_map/ppermute | solution.py:12
  8.3 0.7 collective-permute-start.30
  9.0 1.1 %fusion.20 = (f32[8,8,2048]{2,1,0:T(8,128)S(1)}, f32[8,8,2048]{2,1,0:T(8,128)S(1)}) fusion(bf16[8,8,4096]{2,1,0:T(8,128)(2,1)} %fusion.1), kind=kLoop, calls=%fused_computation.57 | loop fusion | bytes 2097152 | tf_op jit(solution)/shard_map/slice | solution.py:57
  10.1 0.0 copy-done.1
  10.1 0.7 iota_reduce_fusion.1
  10.9 0.7 broadcast_compare_fusion
  11.6 0.1 rev.3
  11.7 0.6 iota_reduce_fusion
  15.5 0.7 fusion.21
  16.9 15.4 %conditional.2 = (bf16[8,8,4096]{2,1,0:T(8,128)(2,1)}) conditional(s32[]{:T(128)} %bitcast.2, bf16[8,8,4096]{2,1,0:T(8,128)(2,1)} %fusion.1, bf16[8,8,4096]{2,1,0:T(8,128)(2,1)} %fusion.1, bf16[8,8,4096]{2,1,0:T(8,128)(2,1)} %fusion.1, bf16[8,8,4096]{2,1,0:T(8,128)(2,1)} %fusion.1, ...), branch_computations={%region_4.5_spmd, %region_5.6_spmd, %region_6.7_spmd, %region_7.8_... | conditional | bytes 2097200 | solution.py:83
  16.9 0.1 collective-permute-start.10
  17.0 15.2 %collective-permute-done.10 = bf16[8,8,4096]{2,1,0:T(8,128)(2,1)} collective-permute-done((bf16[8,8,4096]{2,1,0:T(8,128)(2,1)}, bf16[8,8,4096]{2,1,0:T(8,128)(2,1)}, u32[]{:S(2)}, u32[]{:S(2)}) %collective-permute-start.10) | collective-permute-done | bytes 524320 | tf_op jit(solution)/shard_map/cond/branch_10_fun/ppermute | solution.py:12
  32.9 15.6 %conditional.3 = (bf16[8,8,4096]{2,1,0:T(8,128)(2,1)}) conditional(s32[]{:T(128)} %bitcast.4, bf16[8,8,4096]{2,1,0:T(8,128)(2,1)} %fusion.1, bf16[8,8,4096]{2,1,0:T(8,128)(2,1)} %fusion.1, bf16[8,8,4096]{2,1,0:T(8,128)(2,1)} %fusion.1, bf16[8,8,4096]{2,1,0:T(8,128)(2,1)} %fusion.1, ...), branch_computations={%region_21.22_spmd, %region_22.23_spmd, %region_23.24_spmd, %regio... | conditional | bytes 2097200 | solution.py:84
  33.0 0.3 collective-permute-start.20
  33.2 15.3 %collective-permute-done.20 = bf16[8,8,4096]{2,1,0:T(8,128)(2,1)} collective-permute-done((bf16[8,8,4096]{2,1,0:T(8,128)(2,1)}, bf16[8,8,4096]{2,1,0:T(8,128)(2,1)}, u32[]{:S(2)}, u32[]{:S(2)}) %collective-permute-start.20) | collective-permute-done | bytes 524320 | tf_op jit(solution)/shard_map/cond/branch_5_fun/ppermute | solution.py:12
  48.5 0.5 fusion.13
  49.0 1.4 %fusion.16 = (f32[8,8,2048]{2,1,0:T(8,128)S(1)}, f32[8,8,2048]{2,1,0:T(8,128)S(1)}, f32[8,8,2048]{2,1,0:T(8,128)S(1)}, f32[8,8,2048]{2,1,0:T(8,128)S(1)}) fusion(bf16[8,8,4096]{2,1,0:T(8,128)(2,1)} %get-tuple-element.109, bf16[8,8,4096]{2,1,0:T(8,128)(2,1)} %get-tuple-element.108), kind=kLoop, calls=%fused_computation.53 | loop fusion | bytes 4194304 | tf_op jit(solution)/shard_map/slice | solution.py:59
  50.5 0.3 fusion.15
  50.8 1.2 %negate_multiply_fusion = (f32[32,64,512]{2,1,0:T(8,128)S(1)}, f32[32,64,512]{2,1,0:T(8,128)S(1)}) fusion(f32[64,512]{1,0:T(8,128)S(1)} %get-tuple-element.102, f32[32,512]{1,0:T(8,128)S(1)} %get-tuple-element.100, f32[64,512]{1,0:T(8,128)S(1)} %get-tuple-element.101, f32[32,512]{1,0:T(8,128)S(1)} %get-tuple-element.99), kind=kLoop, calls=%fused_computation.1 | loop fusion | flops 9437184 | bytes 8781824 | tf_op jit(solution)/shard_map/mul | solution.py:49
  52.0 0.0 collective-permute-done.31
  52.0 0.1 fusion.18
  52.1 0.0 collective-permute-done.30
  52.1 0.1 fusion.19
  52.2 5.8 %subtract_reduce_fusion.3 = (f32[8,8,2048]{2,1,0:T(8,128)S(1)}, f32[8,8,2048]{2,1,0:T(8,128)S(1)}, f32[8,8,2048]{2,1,0:T(8,128)S(1)}, f32[8,8,2048]{2,1,0:T(8,12...) fusion(f32[8,8,2048]{2,1,0:T(8,128)S(1)} %get-tuple-element.96,, ...), kind=kLoop, calls=%fused_computation.5 | loop fusion | flops 32505856 | bytes 9437184 | tf_op jit(solution)/shard_map/reduce_sum | solution.py:62
  58.0 0.1 pad_maximum_fusion.1
  58.1 0.1 copy.5
  58.3 0.1 pad_maximum_fusion
  58.4 0.1 copy.4
  58.6 3.7 %fusion.22 = f32[256,512]{1,0:T(8,128)S(1)} fusion(f32[256,2048]{1,0:T(8,128)S(1)} %bitcast.27, f32[2048,512]{1,0:T(8,128)S(1)} %bitcast.25), kind=kOutput, calls=%fused_computation.59 | convolution fusion | flops 3221225472 | bytes 6815744 | tf_op jit(solution)/shard_map/dot_general | solution.py:94
  62.3 4.5 %convolution_add_fusion = f32[256,512]{1,0:T(8,128)} fusion(f32[256,512]{1,0:T(8,128)S(1)} %fusion.22, f32[256,2048]{1,0:T(8,128)S(1)} %bitcast.26, f32[2048,512]{1,0:T(8,128)S(1)} %bitcast.24), kind=kOutput, calls=%fused_computation.13 | convolution fusion | flops 3221356544 | bytes 7340032 | tf_op jit(solution)/shard_map/dot_general | solution.py:95
  66.8 6.8 %all-to-all-start = ((f32[8,32,512]{2,1,0:T(8,128)}), f32[8,32,512]{2,1,0:T(8,128)S(1)}, u32[]{:S(2)}, u32[]{:S(2)}) async-start(f32[8,32,512]{2,1,0:T(8,128)} %bitcast.14), calls=%async_computation | async-start | bytes 1048576 | tf_op jit(solution)/shard_map/all_to_all | solution.py:100
  73.6 11.0 %all-to-all-done = f32[8,32,512]{2,1,0:T(8,128)S(1)} async-done(((f32[8,32,512]{2,1,0:T(8,128)}), f32[8,32,512]{2,1,0:T(8,128)S(1)}, u32[]{:S(2)}, u32[]{:S(2)}) %all-to-all-start) | async-done | bytes 524320 | tf_op jit(solution)/shard_map/all_to_all | solution.py:100
  84.7 0.6 gather_fusion
  85.3 0.7 bitcast_select_fusion
  (6 shorter events, 0.1 us)
Async XLA Ops:
  0.0 2.8 %copy-start = (bf16[8,8,4096]{2,1,0:T(8,128)(2,1)S(1)}, bf16[8,8,4096]{2,1,0:T(8,128)(2,1)}, u32[]{:S(2)}) copy-start(bf16[8,8,4096]{2,1,0:T(8,128)(2,1)} %param.33) | copy-start | bytes 1572868
  0.0 2.8 %copy-start.2 = (s32[8]{0:T(128)S(1)}, s32[8]{0:T(128)}, u32[]{:S(2)}) copy-start(s32[8]{0:T(128)} %param.34) | copy-start | bytes 100
  1.3 8.9 %copy-start.1 = (s32[4]{0:T(128)S(1)}, s32[4]{0:T(128)}, u32[]{:S(2)}) copy-start(s32[4]{0:T(128)} %param.35) | copy-start | bytes 52
  3.7 48.3 %collective-permute-start.31 = (bf16[8,8,4096]{2,1,0:T(8,128)(2,1)}, bf16[8,8,4096]{2,1,0:T(8,128)(2,1)S(1)}, u32[]{:S(2)}, u32[]{:S(2)}) collective-permute-start(bf16[8,8,4096]{2,1,0:T(8,128)(2,1)} %fusion.1), channel_id=1, source_target_pairs={{0,120},{8,112},{16,104},{24,96},{32,88},{40,80},{48,72},{56,64},{... | collective-permute-start | bytes 1572872 | tf_op jit(solution)/shard_map/ppermute | solution.py:12
  8.3 43.8 %collective-permute-start.30 = (bf16[8,8,4096]{2,1,0:T(8,128)(2,1)}, bf16[8,8,4096]{2,1,0:T(8,128)(2,1)S(1)}, u32[]{:S(2)}, u32[]{:S(2)}) collective-permute-start(bf16[8,8,4096]{2,1,0:T(8,128)(2,1)} %fusion.1), channel_id=1, source_target_pairs={{0,8},{8,0},{16,24},{24,16},{32,40},{40,32},{48,56},{56,48},{64,72... | collective-permute-start | bytes 1572872 | tf_op jit(solution)/shard_map/ppermute | solution.py:12
  16.9 15.3 %collective-permute-start.10 = (bf16[8,8,4096]{2,1,0:T(8,128)(2,1)}, bf16[8,8,4096]{2,1,0:T(8,128)(2,1)}, u32[]{:S(2)}, u32[]{:S(2)}) collective-permute-start(bf16[8,8,4096]{2,1,0:T(8,128)(2,1)} %param.10), channel_id=1, source_target_pairs={{0,88},{8,80},{16,72},{24,64},{32,120},{40,112},{48,104},{56,96},{... | collective-permute-start | bytes 1572872 | tf_op jit(solution)/shard_map/cond/branch_10_fun/ppermute | solution.py:12
  33.0 15.6 %collective-permute-start.20 = (bf16[8,8,4096]{2,1,0:T(8,128)(2,1)}, bf16[8,8,4096]{2,1,0:T(8,128)(2,1)}, u32[]{:S(2)}, u32[]{:S(2)}) collective-permute-start(bf16[8,8,4096]{2,1,0:T(8,128)(2,1)} %param.20), channel_id=1, source_target_pairs={{0,48},{8,56},{16,32},{24,40},{32,16},{40,24},{48,0},{56,8},{64,11... | collective-permute-start | bytes 1572872 | tf_op jit(solution)/shard_map/cond/branch_5_fun/ppermute | solution.py:12
  66.8 17.9 %all-to-all-start = ((f32[8,32,512]{2,1,0:T(8,128)}), f32[8,32,512]{2,1,0:T(8,128)S(1)}, u32[]{:S(2)}, u32[]{:S(2)}) async-start(f32[8,32,512]{2,1,0:T(8,128)} %bitcast.14), calls=%async_computation | async-start | bytes 1048576 | tf_op jit(solution)/shard_map/all_to_all | solution.py:100

commit v3 on v2

--- a/solution.py
+++ b/solution.py
@@ -77,28 +77,38 @@
     branches = [
         (lambda v, m=m: xor_permute(v, "chan", m)) for m in range(1, n_chan)
     ]
+    hp = lax.Precision.HIGHEST
+
+    def lags_of(partners):
+        re_parts, im_parts = [], []
+        for partner in partners:
+            cross_re, cross_im = cross_spectrum(own_block, partner)
+            re_parts.append(cross_re)
+            im_parts.append(cross_im)
+        cross_re = jnp.stack(re_parts, axis=1).reshape(-1, n_freq)
+        cross_im = jnp.stack(im_parts, axis=1).reshape(-1, n_freq)
+        lagged = jnp.dot(cross_re, cos_t, precision=hp, preferred_element_type=jnp.float32)
+        lagged = lagged + jnp.dot(
+            cross_im, neg_sin_t, precision=hp, preferred_element_type=jnp.float32
+        )
+        return lagged.reshape(chans, len(partners) * chans, LAGS)
+
+    def hour_sum(lagged):
+        gathered = lax.all_to_all(lagged, "hour", 0, 0, tiled=True)
+        return jnp.sum(gathered, axis=0)
+
+    switched_a = lax.switch(plan[first] - 1, branches, own_block)
+    next_block, _ = lax.optimization_barrier((own_block, switched_a))
+    switched_b = lax.switch(plan[last] - 1, branches, next_block)
+    late_block, _ = lax.optimization_barrier((own_block, switched_b))
     partners = [
-        xor_permute(own_block, "chan", 1),
-        xor_permute(own_block, "chan", n_chan - 1),
-        lax.switch(plan[first] - 1, branches, own_block),
-        lax.switch(plan[last] - 1, branches, own_block),
+        xor_permute(late_block, "chan", 1),
+        xor_permute(late_block, "chan", n_chan - 1),
+        switched_a,
+        switched_b,
     ]
-    re_parts, im_parts = [], []
-    for partner in partners:
-        cross_re, cross_im = cross_spectrum(own_block, partner)
-        re_parts.append(cross_re)
-        im_parts.append(cross_im)
-    cross_re = jnp.stack(re_parts, axis=1).reshape(-1, n_freq)
-    cross_im = jnp.stack(im_parts, axis=1).reshape(-1, n_freq)
-    hp = lax.Precision.HIGHEST
-    lagged = jnp.dot(cross_re, cos_t, precision=hp, preferred_element_type=jnp.float32)
-    lagged = lagged + jnp.dot(
-        cross_im, neg_sin_t, precision=hp, preferred_element_type=jnp.float32
-    )
-    lagged = lagged.reshape(chans, ROUNDS * chans, LAGS)
-
-    gathered = lax.all_to_all(lagged, "hour", 0, 0, tiled=True)
-    total = jnp.sum(gathered, axis=0).reshape(ROUNDS, chans, LAGS)
+    lagged = lags_of(partners)
+    total = hour_sum(lagged).reshape(ROUNDS, chans, LAGS)
 
     slot = jnp.where(
         plan == 1,

time: 86.1 us -> 94.6 us (1.099); the launches traced: 86 us -> 93 us
  starting transfers between devices: 12.5 us -> 17.8 us
  waiting for transfers between devices: 41.5 us -> 43.7 us
  local copies, waits for them, and re-layouts: 5.46 us -> 4.44 us
    ppermute x4, starting transfers between devices: 5.63 us -> 10.6 us  [xor_permute(): lax.ppermute(value, axis, [(i, i ^ mask) for i in range(lax.axis_size(axi...]
    ppermute x4, waiting for transfers between devices: 30.5 us -> 31.9 us  [xor_permute(): lax.ppermute(value, axis, [(i, i ^ mask) for i in range(lax.axis_size(axi...]
    slice x1, local copies, waits for them, and re-layouts: 1.12 us -> 0.09 us  [cross_spectrum(): a_re = a[:, None, :, :n_freq]]
  transfers between devices with their start and end apart: 5 -> 5, of which waited for: 3 -> 4; matrix products, arithmetic and copies ran while one was open for 9% -> 4% of each run, Pallas kernels for 0% -> 0%
where the time goes in v3:
time: 94.6 us; the launch traced here: 93 us
  waiting for transfers between devices  43.7 us (46%)
  starting transfers between devices  17.8 us (19%)
  other arithmetic  14 us (15%)
  matrix products  8.19 us (9%)
  between operations  4.79 us (5%)
  local copies, waits for them, and re-layouts  4.44 us (5%)
    ppermute x4, waiting for transfers between devices, xor_permute(): lax.ppermute(value, axis, [(i, i ^ mask) for i in range(lax.axis_size(axi...  31.9 us
    all_to_all x1, waiting for transfers between devices, hour_sum(): gathered = lax.all_to_all(lagged, 'hour', 0, 0, tiled=True)  11.9 us
    ppermute x4, starting transfers between devices, xor_permute(): lax.ppermute(value, axis, [(i, i ^ mask) for i in range(lax.axis_size(axi...  10.6 us
    all_to_all x1, starting transfers between devices, hour_sum(): gathered = lax.all_to_all(lagged, 'hour', 0, 0, tiled=True)  7.16 us
    reduce_sum x1, other arithmetic, cross_spectrum(): cross_im = jnp.sum(b_re * a_im - b_im * a_re, axis=0)  5.77 us
    dot_general x1, matrix products, lags_of(): jnp.dot(cross_im, neg_sin_t, precision=hp, preferred_element_type=jnp.flo...  4.51 us
    dot_general x1, matrix products, lags_of(): jnp.dot(cross_re, cos_t, precision=hp, preferred_element_type=jnp.float32)  3.69 us
    another operation x2, other arithmetic, per_device(): first = jnp.argmax(others).astype(jnp.int32)  2.03 us
  transfers between devices with their start and end apart: 5, of which 4 were waited for; matrix products, arithmetic and copies ran while one was open for 4% of the time, Pallas kernels for 0%

profile of v3, /device:TPU:0, one launch (start us, length us, event | category | flops | bytes accessed | tf_op | source)
XLA Modules:
  0.0 93.0 jit_solution(652430895685721697)
XLA Ops:
  0.0 1.4 %iota_reduce_fusion.1 = (pred[]{:T(512)}, s32[]{:T(128)}) fusion(s32[4]{0:T(128)} %param.35), kind=kLoop, calls=%fused_computation.51 | loop fusion | flops 33 | bytes 21 | tf_op jit(solution)/shard_map/per_device/reduce | solution.py:75
  1.4 1.4 %broadcast_compare_fusion = (pred[4]{0:T(512)(128)(4,1)S(1)}, s32[4]{0:T(128)S(1)}, pred[4]{0:T(512)(128)(4,1)S(1)}) fusion(s32[]{:T(128)} %get-tuple-element.71, s32[4]{0:T(128)} %param.35), kind=kLoop, calls=%fused_computation.52 | loop fusion | flops 40 | bytes 44 | tf_op jit(solution)/shard_map/jit(_take)/le | solution.py:122
  2.7 0.1 rev.3
  2.8 0.6 iota_reduce_fusion
  6.0 0.0 copy-start.2
  6.0 0.0 copy-start.1
  6.0 0.0 copy-start
  6.0 1.2 %convert_element_type.96 = f32[8,8,4096]{2,1,0:T(8,128)S(1)} convert(bf16[8,8,4096]{2,1,0:T(8,128)(2,1)} %param.33) | non-fusion elementwise | flops 262144 | bytes 1572864 | tf_op jit(solution)/shard_map/convert_element_type | solution.py:18
  7.2 0.1 fusion.2
  7.3 0.4 reshape.223
  7.7 0.3 reduce_sum.90
  8.1 0.3 broadcast_in_dim.25
  8.4 0.4 reshape.224
  8.8 0.0 copy-done.2
  9.5 0.0 copy-done.1
  9.5 0.7 fusion.21
  10.8 0.0 copy-done
  10.8 0.2 fusion.1
  11.0 16.1 %conditional.2 = (bf16[8,8,4096]{2,1,0:T(8,128)(2,1)}) conditional(s32[]{:T(128)} %bitcast.1, bf16[8,8,4096]{2,1,0:T(8,128)(2,1)S(1)} %fusion.1, bf16[8,8,4096]{2,1,0:T(8,128)(2,1)S(1)} %fusion.1, bf16[8,8,4096]{2,1,0:T(8,128)(2,1)S(1)} %fusion.1, bf16[8,8,4096]{2,1,0:T(8,128)(2,1)S(1)} %fusion.1, ...), branch_computations={%region_3.4_spmd, %region_4.5_spmd, %region_5.6_spmd, %region_6.7_... | conditional | bytes 2097200 | solution.py:100
  11.0 4.0 %collective-permute-start.3 = (bf16[8,8,4096]{2,1,0:T(8,128)(2,1)S(1)}, bf16[8,8,4096]{2,1,0:T(8,128)(2,1)}, u32[]{:S(2)}, u32[]{:S(2)}) collective-permute-start(bf16[8,8,4096]{2,1,0:T(8,128)(2,1)S(1)} %param.3), channel_id=1, source_target_pairs={{0,32},{8,40},{16,48},{24,56},{32,0},{40,8},{48,16},{56,24},{64,96... | collective-permute-start | bytes 1572872 | tf_op jit(solution)/shard_map/cond/branch_3_fun/ppermute | solution.py:12
  15.1 12.0 %collective-permute-done.3 = bf16[8,8,4096]{2,1,0:T(8,128)(2,1)} collective-permute-done((bf16[8,8,4096]{2,1,0:T(8,128)(2,1)S(1)}, bf16[8,8,4096]{2,1,0:T(8,128)(2,1)}, u32[]{:S(2)}, u32[]{:S(2)}) %collective-permute-start.3) | collective-permute-done | bytes 524320 | tf_op jit(solution)/shard_map/cond/branch_3_fun/ppermute | solution.py:12
  27.8 14.2 %conditional.3 = (bf16[8,8,4096]{2,1,0:T(8,128)(2,1)}) conditional(s32[]{:T(128)} %bitcast, bf16[8,8,4096]{2,1,0:T(8,128)(2,1)S(1)} %fusion.1, bf16[8,8,4096]{2,1,0:T(8,128)(2,1)S(1)} %fusion.1, bf16[8,8,4096]{2,1,0:T(8,128)(2,1)S(1)} %fusion.1, bf16[8,8,4096]{2,1,0:T(8,128)(2,1)S(1)} %fusion.1, ...), branch_computations={%region_18.19_spmd, %region_19.20_spmd, %region_20.21_spmd, %regio... | conditional | bytes 2097200 | solution.py:102
  27.8 2.4 %collective-permute-start.24 = (bf16[8,8,4096]{2,1,0:T(8,128)(2,1)S(1)}, bf16[8,8,4096]{2,1,0:T(8,128)(2,1)}, u32[]{:S(2)}, u32[]{:S(2)}) collective-permute-start(bf16[8,8,4096]{2,1,0:T(8,128)(2,1)S(1)} %param.24), channel_id=1, source_target_pairs={{0,80},{8,88},{16,64},{24,72},{32,112},{40,120},{48,96},{56,104},{... | collective-permute-start | bytes 1572872 | tf_op jit(solution)/shard_map/cond/branch_9_fun/ppermute | solution.py:12
  30.2 11.8 %collective-permute-done.24 = bf16[8,8,4096]{2,1,0:T(8,128)(2,1)} collective-permute-done((bf16[8,8,4096]{2,1,0:T(8,128)(2,1)S(1)}, bf16[8,8,4096]{2,1,0:T(8,128)(2,1)}, u32[]{:S(2)}, u32[]{:S(2)}) %collective-permute-start.24) | collective-permute-done | bytes 524320 | tf_op jit(solution)/shard_map/cond/branch_9_fun/ppermute | solution.py:12
  42.0 1.7 %collective-permute-start.31 = (bf16[8,8,4096]{2,1,0:T(8,128)(2,1)S(1)}, bf16[8,8,4096]{2,1,0:T(8,128)(2,1)S(1)}, u32[]{:S(2)}, u32[]{:S(2)}) collective-permute-start(bf16[8,8,4096]{2,1,0:T(8,128)(2,1)S(1)} %fusion.1), channel_id=1, source_target_pairs={{0,120},{8,112},{16,104},{24,96},{32,88},{40,80},{48,72},{56,64},{... | collective-permute-start | bytes 1572872 | tf_op jit(solution)/shard_map/ppermute | solution.py:12
  43.8 2.5 %collective-permute-start.30 = (bf16[8,8,4096]{2,1,0:T(8,128)(2,1)S(1)}, bf16[8,8,4096]{2,1,0:T(8,128)(2,1)S(1)}, u32[]{:S(2)}, u32[]{:S(2)}) collective-permute-start(bf16[8,8,4096]{2,1,0:T(8,128)(2,1)S(1)} %fusion.1), channel_id=1, source_target_pairs={{0,8},{8,0},{16,24},{24,16},{32,40},{40,32},{48,56},{56,48},{64,72... | collective-permute-start | bytes 1572872 | tf_op jit(solution)/shard_map/ppermute | solution.py:12
  46.2 1.4 %fusion.16 = (f32[8,8,2048]{2,1,0:T(8,128)S(1)}, f32[8,8,2048]{2,1,0:T(8,128)S(1)}, f32[8,8,2048]{2,1,0:T(8,128)S(1)}, f32[8,8,2048]{2,1,0:T(8,128)S(1)}) fusion(bf16[8,8,4096]{2,1,0:T(8,128)(2,1)} %get-tuple-element.113, bf16[8,8,4096]{2,1,0:T(8,128)(2,1)} %get-tuple-element.112), kind=kLoop, calls=%fused_computation.53 | loop fusion | bytes 4194304 | tf_op jit(solution)/shard_map/slice | solution.py:59
  47.7 0.1 fusion.20
  47.8 0.5 fusion.13
  48.3 0.3 fusion.15
  48.7 1.2 %negate_multiply_fusion = (f32[32,64,512]{2,1,0:T(8,128)S(1)}, f32[32,64,512]{2,1,0:T(8,128)S(1)}) fusion(f32[64,512]{1,0:T(8,128)S(1)} %get-tuple-element.106, f32[32,512]{1,0:T(8,128)S(1)} %get-tuple-element.104, f32[64,512]{1,0:T(8,128)S(1)} %get-tuple-element.105, f32[32,512]{1,0:T(8,128)S(1)} %get-tuple-element.103), kind=kLoop, calls=%fused_computation.1 | loop fusion | flops 9437184 | bytes 8781824 | tf_op jit(solution)/shard_map/mul | solution.py:49
  49.8 8.0 %collective-permute-done.31 = bf16[8,8,4096]{2,1,0:T(8,128)(2,1)S(1)} collective-permute-done((bf16[8,8,4096]{2,1,0:T(8,128)(2,1)S(1)}, bf16[8,8,4096]{2,1,0:T(8,128)(2,1)S(1)}, u32[]{:S(2)}, u32[]{:S(2)}) %collective-permute-start.31) | collective-permute-done | bytes 524320 | tf_op jit(solution)/shard_map/ppermute | solution.py:12
  57.9 0.1 fusion.18
  58.0 0.0 collective-permute-done.30
  58.0 0.1 fusion.19
  58.1 5.8 %subtract_reduce_fusion.3 = (f32[8,8,2048]{2,1,0:T(8,128)S(1)}, f32[8,8,2048]{2,1,0:T(8,128)S(1)}, f32[8,8,2048]{2,1,0:T(8,128)S(1)}, f32[8,8,2048]{2,1,0:T(8,12...) fusion(f32[8,8,2048]{2,1,0:T(8,128)S(1)} %get-tuple-element.100, ...), kind=kLoop, calls=%fused_computation.5 | loop fusion | flops 32505856 | bytes 9437184 | tf_op jit(solution)/shard_map/reduce_sum | solution.py:62
  63.9 0.1 pad_maximum_fusion.1
  64.0 0.1 copy.5
  64.2 0.1 pad_maximum_fusion
  64.3 0.1 copy.4
  64.5 3.7 %fusion.22 = f32[256,512]{1,0:T(8,128)S(1)} fusion(f32[256,2048]{1,0:T(8,128)S(1)} %bitcast.27, f32[2048,512]{1,0:T(8,128)S(1)} %bitcast.25), kind=kOutput, calls=%fused_computation.59 | convolution fusion | flops 3221225472 | bytes 6815744 | tf_op jit(solution)/shard_map/dot_general | solution.py:90
  68.2 4.5 %convolution_add_fusion = f32[256,512]{1,0:T(8,128)} fusion(f32[256,512]{1,0:T(8,128)S(1)} %fusion.22, f32[256,2048]{1,0:T(8,128)S(1)} %bitcast.26, f32[2048,512]{1,0:T(8,128)S(1)} %bitcast.24), kind=kOutput, calls=%fused_computation.13 | convolution fusion | flops 3221356544 | bytes 7340032 | tf_op jit(solution)/shard_map/dot_general | solution.py:91
  72.7 7.2 %all-to-all-start = ((f32[8,32,512]{2,1,0:T(8,128)}), f32[8,32,512]{2,1,0:T(8,128)S(1)}, u32[]{:S(2)}, u32[]{:S(2)}) async-start(f32[8,32,512]{2,1,0:T(8,128)} %bitcast.14), calls=%async_computation | async-start | bytes 1048576 | tf_op jit(solution)/shard_map/all_to_all | solution.py:97
  79.8 11.9 %all-to-all-done = f32[8,32,512]{2,1,0:T(8,128)S(1)} async-done(((f32[8,32,512]{2,1,0:T(8,128)}), f32[8,32,512]{2,1,0:T(8,128)S(1)}, u32[]{:S(2)}, u32[]{:S(2)}) %all-to-all-start) | async-done | bytes 524320 | tf_op jit(solution)/shard_map/all_to_all | solution.py:97
  91.7 0.6 gather_fusion
  92.3 0.7 bitcast_select_fusion
  (6 shorter events, 0.1 us)
Async XLA Ops:
  6.0 2.8 %copy-start.2 = (s32[8]{0:T(128)S(1)}, s32[8]{0:T(128)}, u32[]{:S(2)}) copy-start(s32[8]{0:T(128)} %param.34) | copy-start | bytes 100
  6.0 3.5 %copy-start.1 = (s32[4]{0:T(128)S(1)}, s32[4]{0:T(128)}, u32[]{:S(2)}) copy-start(s32[4]{0:T(128)} %param.35) | copy-start | bytes 52
  6.0 4.8 %copy-start = (bf16[8,8,4096]{2,1,0:T(8,128)(2,1)S(1)}, bf16[8,8,4096]{2,1,0:T(8,128)(2,1)}, u32[]{:S(2)}) copy-start(bf16[8,8,4096]{2,1,0:T(8,128)(2,1)} %param.33) | copy-start | bytes 1572868
  11.0 16.1 %collective-permute-start.3 = (bf16[8,8,4096]{2,1,0:T(8,128)(2,1)S(1)}, bf16[8,8,4096]{2,1,0:T(8,128)(2,1)}, u32[]{:S(2)}, u32[]{:S(2)}) collective-permute-start(bf16[8,8,4096]{2,1,0:T(8,128)(2,1)S(1)} %param.3), channel_id=1, source_target_pairs={{0,32},{8,40},{16,48},{24,56},{32,0},{40,8},{48,16},{56,24},{64,96... | collective-permute-start | bytes 1572872 | tf_op jit(solution)/shard_map/cond/branch_3_fun/ppermute | solution.py:12
  27.8 14.2 %collective-permute-start.24 = (bf16[8,8,4096]{2,1,0:T(8,128)(2,1)S(1)}, bf16[8,8,4096]{2,1,0:T(8,128)(2,1)}, u32[]{:S(2)}, u32[]{:S(2)}) collective-permute-start(bf16[8,8,4096]{2,1,0:T(8,128)(2,1)S(1)} %param.24), channel_id=1, source_target_pairs={{0,80},{8,88},{16,64},{24,72},{32,112},{40,120},{48,96},{56,104},{... | collective-permute-start | bytes 1572872 | tf_op jit(solution)/shard_map/cond/branch_9_fun/ppermute | solution.py:12
  42.0 15.9 %collective-permute-start.31 = (bf16[8,8,4096]{2,1,0:T(8,128)(2,1)S(1)}, bf16[8,8,4096]{2,1,0:T(8,128)(2,1)S(1)}, u32[]{:S(2)}, u32[]{:S(2)}) collective-permute-start(bf16[8,8,4096]{2,1,0:T(8,128)(2,1)S(1)} %fusion.1), channel_id=1, source_target_pairs={{0,120},{8,112},{16,104},{24,96},{32,88},{40,80},{48,72},{56,64},{... | collective-permute-start | bytes 1572872 | tf_op jit(solution)/shard_map/ppermute | solution.py:12
  43.8 14.2 %collective-permute-start.30 = (bf16[8,8,4096]{2,1,0:T(8,128)(2,1)S(1)}, bf16[8,8,4096]{2,1,0:T(8,128)(2,1)S(1)}, u32[]{:S(2)}, u32[]{:S(2)}) collective-permute-start(bf16[8,8,4096]{2,1,0:T(8,128)(2,1)S(1)} %fusion.1), channel_id=1, source_target_pairs={{0,8},{8,0},{16,24},{24,16},{32,40},{40,32},{48,56},{56,48},{64,72... | collective-permute-start | bytes 1572872 | tf_op jit(solution)/shard_map/ppermute | solution.py:12
  72.7 19.0 %all-to-all-start = ((f32[8,32,512]{2,1,0:T(8,128)}), f32[8,32,512]{2,1,0:T(8,128)S(1)}, u32[]{:S(2)}, u32[]{:S(2)}) async-start(f32[8,32,512]{2,1,0:T(8,128)} %bitcast.14), calls=%async_computation | async-start | bytes 1048576 | tf_op jit(solution)/shard_map/all_to_all | solution.py:97

commit v4 on v2

--- a/solution.py
+++ b/solution.py
@@ -90,7 +90,7 @@
         im_parts.append(cross_im)
     cross_re = jnp.stack(re_parts, axis=1).reshape(-1, n_freq)
     cross_im = jnp.stack(im_parts, axis=1).reshape(-1, n_freq)
-    hp = lax.Precision.HIGHEST
+    hp = lax.Precision.HIGH
     lagged = jnp.dot(cross_re, cos_t, precision=hp, preferred_element_type=jnp.float32)
     lagged = lagged + jnp.dot(
         cross_im, neg_sin_t, precision=hp, preferred_element_type=jnp.float32

time: 86.1 us -> 84.8 us (0.985)
  matrix products: 8.19 us -> 5.36 us
  waiting for transfers between devices: 41.5 us -> 42.9 us
    dot_general x1, matrix products: 4.51 us -> 3.09 us  [per_device(): jnp.dot(cross_im, neg_sin_t, precision=hp, preferred_element_type=jnp.flo...]
    dot_general x1, matrix products: 3.69 us -> 2.28 us  [per_device(): jnp.dot(cross_re, cos_t, precision=hp, preferred_element_type=jnp.float32)]
    ppermute x4, waiting for transfers between devices: 30.5 us -> 31.9 us  [xor_permute(): lax.ppermute(value, axis, [(i, i ^ mask) for i in range(lax.axis_size(axi...]
where the time goes in v4:
time: 84.8 us; the launch traced here: 84.1 us
  waiting for transfers between devices  42.9 us (51%)
  other arithmetic  13.5 us (16%)
  starting transfers between devices  12.1 us (14%)
  local copies, waits for them, and re-layouts  5.46 us (6%)
  matrix products  5.36 us (6%)
  between operations  4.79 us (6%)
    ppermute x4, waiting for transfers between devices, xor_permute(): lax.ppermute(value, axis, [(i, i ^ mask) for i in range(lax.axis_size(axi...  31.9 us
    all_to_all x1, waiting for transfers between devices, per_device(): gathered = lax.all_to_all(lagged, 'hour', 0, 0, tiled=True)  11 us
    all_to_all x1, starting transfers between devices, per_device(): gathered = lax.all_to_all(lagged, 'hour', 0, 0, tiled=True)  6.65 us
    reduce_sum x1, other arithmetic, cross_spectrum(): cross_im = jnp.sum(b_re * a_im - b_im * a_re, axis=0)  5.78 us
    ppermute x4, starting transfers between devices, xor_permute(): lax.ppermute(value, axis, [(i, i ^ mask) for i in range(lax.axis_size(axi...  5.42 us
    dot_general x1, matrix products, per_device(): jnp.dot(cross_im, neg_sin_t, precision=hp, preferred_element_type=jnp.flo...  3.09 us
    dot_general x1, matrix products, per_device(): jnp.dot(cross_re, cos_t, precision=hp, preferred_element_type=jnp.float32)  2.28 us
  transfers between devices with their start and end apart: 5, of which 3 were waited for; matrix products, arithmetic and copies ran while one was open for 9% of the time, Pallas kernels for 0%

profile of v4, /device:TPU:0, one launch (start us, length us, event | category | flops | bytes accessed | tf_op | source)
XLA Modules:
  0.0 84.1 jit_solution(4204044293409947032)
XLA Ops:
  0.0 0.0 copy-start
  0.0 0.0 copy-start.2
  0.0 1.2 %convert_element_type.141 = f32[8,8,4096]{2,1,0:T(8,128)S(1)} convert(bf16[8,8,4096]{2,1,0:T(8,128)(2,1)} %param.33) | non-fusion elementwise | flops 262144 | bytes 1572864 | tf_op jit(solution)/shard_map/convert_element_type | solution.py:18
  1.2 0.1 fusion.2
  1.3 0.0 copy-start.1
  1.3 0.4 reshape.223
  1.7 0.3 reduce_sum.90
  2.1 0.3 broadcast_in_dim.25
  2.4 0.4 reshape.224
  2.8 0.0 copy-done.2
  2.8 0.0 copy-done
  2.8 0.9 %fusion.1 = bf16[8,8,4096]{2,1,0:T(8,128)(2,1)} fusion(f32[8,8,2048]{2,1,0:T(8,128)S(1)} %reshape.224, f32[8]{0:T(128)S(1)} %convert_element_type.142, bf16[8,8,4096]{2,1,0:T(8,128)(2,1)S(1)} %copy-done), kind=kLoop, calls=%fused_computation.16 | loop fusion | flops 1310720 | bytes 1572896 | tf_op jit(solution)/shard_map/convert_element_type | solution.py:31
  3.7 4.6 %collective-permute-start.31 = (bf16[8,8,4096]{2,1,0:T(8,128)(2,1)}, bf16[8,8,4096]{2,1,0:T(8,128)(2,1)S(1)}, u32[]{:S(2)}, u32[]{:S(2)}) collective-permute-start(bf16[8,8,4096]{2,1,0:T(8,128)(2,1)} %fusion.1), channel_id=1, source_target_pairs={{0,120},{8,112},{16,104},{24,96},{32,88},{40,80},{48,72},{56,64},{... | collective-permute-start | bytes 1572872 | tf_op jit(solution)/shard_map/ppermute | solution.py:12
  8.3 0.7 collective-permute-start.30
  9.0 1.1 %fusion.20 = (f32[8,8,2048]{2,1,0:T(8,128)S(1)}, f32[8,8,2048]{2,1,0:T(8,128)S(1)}) fusion(bf16[8,8,4096]{2,1,0:T(8,128)(2,1)} %fusion.1), kind=kLoop, calls=%fused_computation.57 | loop fusion | bytes 2097152 | tf_op jit(solution)/shard_map/slice | solution.py:57
  10.1 0.0 copy-done.1
  10.1 0.7 iota_reduce_fusion.1
  10.9 0.7 broadcast_compare_fusion
  11.6 0.1 rev.3
  11.7 0.6 iota_reduce_fusion
  15.5 0.7 fusion.21
  16.9 16.9 %conditional.2 = (bf16[8,8,4096]{2,1,0:T(8,128)(2,1)}) conditional(s32[]{:T(128)} %bitcast.2, bf16[8,8,4096]{2,1,0:T(8,128)(2,1)} %fusion.1, bf16[8,8,4096]{2,1,0:T(8,128)(2,1)} %fusion.1, bf16[8,8,4096]{2,1,0:T(8,128)(2,1)} %fusion.1, bf16[8,8,4096]{2,1,0:T(8,128)(2,1)} %fusion.1, ...), branch_computations={%region_4.5_spmd, %region_5.6_spmd, %region_6.7_spmd, %region_7.8_... | conditional | bytes 2097200 | solution.py:83
  16.9 0.1 collective-permute-start.12
  17.0 16.7 %collective-permute-done.12 = bf16[8,8,4096]{2,1,0:T(8,128)(2,1)} collective-permute-done((bf16[8,8,4096]{2,1,0:T(8,128)(2,1)}, bf16[8,8,4096]{2,1,0:T(8,128)(2,1)}, u32[]{:S(2)}, u32[]{:S(2)}) %collective-permute-start.12) | collective-permute-done | bytes 524320 | tf_op jit(solution)/shard_map/cond/branch_12_fun/ppermute | solution.py:12
  34.4 15.3 %conditional.3 = (bf16[8,8,4096]{2,1,0:T(8,128)(2,1)}) conditional(s32[]{:T(128)} %bitcast.4, bf16[8,8,4096]{2,1,0:T(8,128)(2,1)} %fusion.1, bf16[8,8,4096]{2,1,0:T(8,128)(2,1)} %fusion.1, bf16[8,8,4096]{2,1,0:T(8,128)(2,1)} %fusion.1, bf16[8,8,4096]{2,1,0:T(8,128)(2,1)} %fusion.1, ...), branch_computations={%region_21.22_spmd, %region_22.23_spmd, %region_23.24_spmd, %regio... | conditional | bytes 2097200 | solution.py:84
  34.5 0.1 collective-permute-start.24
  34.6 15.1 %collective-permute-done.24 = bf16[8,8,4096]{2,1,0:T(8,128)(2,1)} collective-permute-done((bf16[8,8,4096]{2,1,0:T(8,128)(2,1)}, bf16[8,8,4096]{2,1,0:T(8,128)(2,1)}, u32[]{:S(2)}, u32[]{:S(2)}) %collective-permute-start.24) | collective-permute-done | bytes 524320 | tf_op jit(solution)/shard_map/cond/branch_9_fun/ppermute | solution.py:12
  49.7 0.5 fusion.13
  50.2 1.4 %fusion.16 = (f32[8,8,2048]{2,1,0:T(8,128)S(1)}, f32[8,8,2048]{2,1,0:T(8,128)S(1)}, f32[8,8,2048]{2,1,0:T(8,128)S(1)}, f32[8,8,2048]{2,1,0:T(8,128)S(1)}) fusion(bf16[8,8,4096]{2,1,0:T(8,128)(2,1)} %get-tuple-element.109, bf16[8,8,4096]{2,1,0:T(8,128)(2,1)} %get-tuple-element.108), kind=kLoop, calls=%fused_computation.53 | loop fusion | bytes 4194304 | tf_op jit(solution)/shard_map/slice | solution.py:59
  51.7 0.3 fusion.15
  52.0 1.2 %negate_multiply_fusion = (f32[32,64,512]{2,1,0:T(8,128)S(1)}, f32[32,64,512]{2,1,0:T(8,128)S(1)}) fusion(f32[64,512]{1,0:T(8,128)S(1)} %get-tuple-element.102, f32[32,512]{1,0:T(8,128)S(1)} %get-tuple-element.100, f32[64,512]{1,0:T(8,128)S(1)} %get-tuple-element.101, f32[32,512]{1,0:T(8,128)S(1)} %get-tuple-element.99), kind=kLoop, calls=%fused_computation.1 | loop fusion | flops 9437184 | bytes 8781824 | tf_op jit(solution)/shard_map/mul | solution.py:49
  53.2 0.0 collective-permute-done.31
  53.2 0.1 fusion.18
  53.3 0.0 collective-permute-done.30
  53.3 0.1 fusion.19
  53.4 5.8 %subtract_reduce_fusion.3 = (f32[8,8,2048]{2,1,0:T(8,128)S(1)}, f32[8,8,2048]{2,1,0:T(8,128)S(1)}, f32[8,8,2048]{2,1,0:T(8,128)S(1)}, f32[8,8,2048]{2,1,0:T(8,12...) fusion(f32[8,8,2048]{2,1,0:T(8,128)S(1)} %get-tuple-element.96,, ...), kind=kLoop, calls=%fused_computation.5 | loop fusion | flops 32505856 | bytes 9437184 | tf_op jit(solution)/shard_map/reduce_sum | solution.py:62
  59.2 0.1 pad_maximum_fusion.1
  59.3 0.1 copy.5
  59.5 0.1 pad_maximum_fusion
  59.6 0.1 copy.4
  59.8 2.3 %fusion.22 = f32[256,512]{1,0:T(8,128)S(1)} fusion(f32[256,2048]{1,0:T(8,128)S(1)} %bitcast.27, f32[2048,512]{1,0:T(8,128)S(1)} %bitcast.25), kind=kOutput, calls=%fused_computation.59 | convolution fusion | flops 1610612736 | bytes 6815744 | tf_op jit(solution)/shard_map/dot_general | solution.py:94
  62.1 3.1 %convolution_add_fusion = f32[256,512]{1,0:T(8,128)} fusion(f32[256,512]{1,0:T(8,128)S(1)} %fusion.22, f32[256,2048]{1,0:T(8,128)S(1)} %bitcast.26, f32[2048,512]{1,0:T(8,128)S(1)} %bitcast.24), kind=kOutput, calls=%fused_computation.13 | convolution fusion | flops 1610743808 | bytes 7340032 | tf_op jit(solution)/shard_map/dot_general | solution.py:95
  65.2 6.6 %all-to-all-start = ((f32[8,32,512]{2,1,0:T(8,128)}), f32[8,32,512]{2,1,0:T(8,128)S(1)}, u32[]{:S(2)}, u32[]{:S(2)}) async-start(f32[8,32,512]{2,1,0:T(8,128)} %bitcast.14), calls=%async_computation | async-start | bytes 1048576 | tf_op jit(solution)/shard_map/all_to_all | solution.py:100
  71.8 11.0 %all-to-all-done = f32[8,32,512]{2,1,0:T(8,128)S(1)} async-done(((f32[8,32,512]{2,1,0:T(8,128)}), f32[8,32,512]{2,1,0:T(8,128)S(1)}, u32[]{:S(2)}, u32[]{:S(2)}) %all-to-all-start) | async-done | bytes 524320 | tf_op jit(solution)/shard_map/all_to_all | solution.py:100
  82.9 0.6 gather_fusion
  83.4 0.7 bitcast_select_fusion
  (6 shorter events, 0.1 us)
Async XLA Ops:
  0.0 2.8 %copy-start = (bf16[8,8,4096]{2,1,0:T(8,128)(2,1)S(1)}, bf16[8,8,4096]{2,1,0:T(8,128)(2,1)}, u32[]{:S(2)}) copy-start(bf16[8,8,4096]{2,1,0:T(8,128)(2,1)} %param.33) | copy-start | bytes 1572868
  0.0 2.8 %copy-start.2 = (s32[8]{0:T(128)S(1)}, s32[8]{0:T(128)}, u32[]{:S(2)}) copy-start(s32[8]{0:T(128)} %param.34) | copy-start | bytes 100
  1.3 8.9 %copy-start.1 = (s32[4]{0:T(128)S(1)}, s32[4]{0:T(128)}, u32[]{:S(2)}) copy-start(s32[4]{0:T(128)} %param.35) | copy-start | bytes 52
  3.7 49.5 %collective-permute-start.31 = (bf16[8,8,4096]{2,1,0:T(8,128)(2,1)}, bf16[8,8,4096]{2,1,0:T(8,128)(2,1)S(1)}, u32[]{:S(2)}, u32[]{:S(2)}) collective-permute-start(bf16[8,8,4096]{2,1,0:T(8,128)(2,1)} %fusion.1), channel_id=1, source_target_pairs={{0,120},{8,112},{16,104},{24,96},{32,88},{40,80},{48,72},{56,64},{... | collective-permute-start | bytes 1572872 | tf_op jit(solution)/shard_map/ppermute | solution.py:12
  8.3 45.0 %collective-permute-start.30 = (bf16[8,8,4096]{2,1,0:T(8,128)(2,1)}, bf16[8,8,4096]{2,1,0:T(8,128)(2,1)S(1)}, u32[]{:S(2)}, u32[]{:S(2)}) collective-permute-start(bf16[8,8,4096]{2,1,0:T(8,128)(2,1)} %fusion.1), channel_id=1, source_target_pairs={{0,8},{8,0},{16,24},{24,16},{32,40},{40,32},{48,56},{56,48},{64,72... | collective-permute-start | bytes 1572872 | tf_op jit(solution)/shard_map/ppermute | solution.py:12
  16.9 16.8 %collective-permute-start.12 = (bf16[8,8,4096]{2,1,0:T(8,128)(2,1)}, bf16[8,8,4096]{2,1,0:T(8,128)(2,1)}, u32[]{:S(2)}, u32[]{:S(2)}) collective-permute-start(bf16[8,8,4096]{2,1,0:T(8,128)(2,1)} %param.12), channel_id=1, source_target_pairs={{0,104},{8,96},{16,120},{24,112},{32,72},{40,64},{48,88},{56,80},{... | collective-permute-start | bytes 1572872 | tf_op jit(solution)/shard_map/cond/branch_12_fun/ppermute | solution.py:12
  34.5 15.2 %collective-permute-start.24 = (bf16[8,8,4096]{2,1,0:T(8,128)(2,1)}, bf16[8,8,4096]{2,1,0:T(8,128)(2,1)}, u32[]{:S(2)}, u32[]{:S(2)}) collective-permute-start(bf16[8,8,4096]{2,1,0:T(8,128)(2,1)} %param.24), channel_id=1, source_target_pairs={{0,80},{8,88},{16,64},{24,72},{32,112},{40,120},{48,96},{56,104},{... | collective-permute-start | bytes 1572872 | tf_op jit(solution)/shard_map/cond/branch_9_fun/ppermute | solution.py:12
  65.2 17.7 %all-to-all-start = ((f32[8,32,512]{2,1,0:T(8,128)}), f32[8,32,512]{2,1,0:T(8,128)S(1)}, u32[]{:S(2)}, u32[]{:S(2)}) async-start(f32[8,32,512]{2,1,0:T(8,128)} %bitcast.14), calls=%async_computation | async-start | bytes 1048576 | tf_op jit(solution)/shard_map/all_to_all | solution.py:100

commit v5 on v3

--- a/solution.py
+++ b/solution.py
@@ -72,12 +72,12 @@
     cos_t, neg_sin_t = lag_table(n_freq, hours * n_hour)
 
     others = (plan != 1) & (plan != n_chan - 1)
-    first = jnp.argmax(others).astype(jnp.int32)
-    last = (ROUNDS - 1 - jnp.argmax(others[::-1])).astype(jnp.int32)
+    low_mask = jnp.min(jnp.where(others, plan, n_chan))
+    high_mask = jnp.max(jnp.where(others, plan, 0))
     branches = [
         (lambda v, m=m: xor_permute(v, "chan", m)) for m in range(1, n_chan)
     ]
-    hp = lax.Precision.HIGHEST
+    hp = lax.Precision.HIGH
 
     def lags_of(partners):
         re_parts, im_parts = [], []
@@ -97,18 +97,18 @@
         gathered = lax.all_to_all(lagged, "hour", 0, 0, tiled=True)
         return jnp.sum(gathered, axis=0)
 
-    switched_a = lax.switch(plan[first] - 1, branches, own_block)
-    next_block, _ = lax.optimization_barrier((own_block, switched_a))
-    switched_b = lax.switch(plan[last] - 1, branches, next_block)
-    late_block, _ = lax.optimization_barrier((own_block, switched_b))
-    partners = [
-        xor_permute(late_block, "chan", 1),
-        xor_permute(late_block, "chan", n_chan - 1),
-        switched_a,
-        switched_b,
+    early = lags_of([
+        xor_permute(own_block, "chan", 1),
+        xor_permute(own_block, "chan", n_chan - 1),
+        lax.switch(low_mask - 1, branches, own_block),
+    ])
+    fetch_and_sum = [
+        (lambda v, e, m=m: (xor_permute(v, "chan", m), hour_sum(e)))
+        for m in range(1, n_chan)
     ]
-    lagged = lags_of(partners)
-    total = hour_sum(lagged).reshape(ROUNDS, chans, LAGS)
+    high_partner, early_sum = lax.switch(high_mask - 1, fetch_and_sum, own_block, early)
+    late_sum = hour_sum(lags_of([high_partner]))
+    total = jnp.concatenate([early_sum, late_sum], axis=0).reshape(ROUNDS, chans, LAGS)
 
     slot = jnp.where(
         plan == 1,
@@ -116,7 +116,7 @@
         jnp.where(
             plan == n_chan - 1,
             1,
-            jnp.where(jnp.arange(ROUNDS, dtype=jnp.int32) == first, 2, 3),
+            jnp.where(plan == low_mask, 2, 3),
         ),
     ).astype(jnp.int32)
     result = jnp.take(total, slot, axis=0)

time: 94.6 us -> 82.7 us (0.87); the launches traced: 93 us -> 84.3 us
  waiting for transfers between devices: 43.7 us -> 21.9 us
  blocking collectives: 0 us -> 18.3 us
  starting transfers between devices: 17.8 us -> 12.4 us
  between operations: 4.79 us -> 1.58 us
  local copies, waits for them, and re-layouts: 4.44 us -> 7.48 us
  other arithmetic: 14 us -> 15 us
    all_to_all x0 -> x1, blocking collectives: none -> 18.3 us  [hour_sum(): gathered = lax.all_to_all(lagged, 'hour', 0, 0, tiled=True)]
    ppermute x4, waiting for transfers between devices: 31.9 us -> 14.5 us  [xor_permute(): lax.ppermute(value, axis, [(i, i ^ mask) for i in range(lax.axis_size(axi...]
    ppermute x4, starting transfers between devices: 10.6 us -> 5.81 us  [xor_permute(): lax.ppermute(value, axis, [(i, i ^ mask) for i in range(lax.axis_size(axi...]
    all_to_all x1, waiting for transfers between devices: 11.9 us -> 7.42 us  [hour_sum(): gathered = lax.all_to_all(lagged, 'hour', 0, 0, tiled=True)]
    mul x1, other arithmetic: 1.17 us -> 4.5 us  [lag_table(): (-(sin_hi * cos_lo + cos_hi * sin_lo)).reshape(n_freq, LAGS) * factor]
    slice x3 -> x4, local copies, waits for them, and re-layouts: 1.62 us -> 3.75 us  [cross_spectrum(): b_re = b[:, :, None, :n_freq]]
    another operation x2 -> x0, other arithmetic: 2.03 us -> none  [per_device(): first = jnp.argmax(others).astype(jnp.int32)]
    unnamed x6 -> x14, local copies, waits for them, and re-layouts: 0.02 us -> 1.86 us
  transfers between devices with their start and end apart: 5 -> 5, of which waited for: 4 -> 3; matrix products, arithmetic and copies ran while one was open for 4% -> 11% of each run, Pallas kernels for 0% -> 0%
where the time goes in v5:
time: 82.7 us; the launch traced here: 84.3 us
  waiting for transfers between devices  21.9 us (26%)
  blocking collectives  18.3 us (22%)
  other arithmetic  15 us (18%)
  starting transfers between devices  12.4 us (15%)
  matrix products  7.54 us (9%)
  local copies, waits for them, and re-layouts  7.48 us (9%)
  between operations  1.58 us (2%)
    all_to_all x1, blocking collectives, hour_sum(): gathered = lax.all_to_all(lagged, 'hour', 0, 0, tiled=True)  18.3 us
    ppermute x4, waiting for transfers between devices, xor_permute(): lax.ppermute(value, axis, [(i, i ^ mask) for i in range(lax.axis_size(axi...  14.5 us
    all_to_all x1, waiting for transfers between devices, hour_sum(): gathered = lax.all_to_all(lagged, 'hour', 0, 0, tiled=True)  7.42 us
    all_to_all x1, starting transfers between devices, hour_sum(): gathered = lax.all_to_all(lagged, 'hour', 0, 0, tiled=True)  6.64 us
    ppermute x4, starting transfers between devices, xor_permute(): lax.ppermute(value, axis, [(i, i ^ mask) for i in range(lax.axis_size(axi...  5.81 us
    reduce_sum x2, other arithmetic, cross_spectrum(): cross_im = jnp.sum(b_re * a_im - b_im * a_re, axis=0)  5.5 us
    mul x1, other arithmetic, lag_table(): (-(sin_hi * cos_lo + cos_hi * sin_lo)).reshape(n_freq, LAGS) * factor  4.5 us
    dot_general x2, matrix products, lags_of(): jnp.dot(cross_im, neg_sin_t, precision=hp, preferred_element_type=jnp.flo...  4.11 us
  transfers between devices with their start and end apart: 5, of which 3 were waited for; matrix products, arithmetic and copies ran while one was open for 11% of the time, Pallas kernels for 0%

profile of v5, /device:TPU:0, one launch (start us, length us, event | category | flops | bytes accessed | tf_op | source)
XLA Modules:
  0.0 84.3 jit_solution(11938804732614353849)
XLA Ops:
  0.0 0.0 copy-start.4
  0.0 0.0 copy-start.6
  0.0 1.2 %convert_element_type.104 = f32[8,8,4096]{2,1,0:T(8,128)S(1)} convert(bf16[8,8,4096]{2,1,0:T(8,128)(2,1)} %param.33) | non-fusion elementwise | flops 262144 | bytes 1572864 | tf_op jit(solution)/shard_map/convert_element_type | solution.py:18
  1.2 0.0 copy-start.5
  1.2 0.1 fusion.3
  1.3 0.4 reshape.224
  1.7 0.3 reduce_sum.225
  2.1 0.3 broadcast_in_dim.31
  2.4 0.4 reshape.225
  2.8 0.0 copy-done.6
  2.8 0.0 copy-done.4
  2.8 0.2 fusion.2
  3.0 4.7 %collective-permute-start.31 = (bf16[8,8,4096]{2,1,0:T(8,128)(2,1)S(1)}, bf16[8,8,4096]{2,1,0:T(8,128)(2,1)}, u32[]{:S(2)}, u32[]{:S(2)}) collective-permute-start(bf16[8,8,4096]{2,1,0:T(8,128)(2,1)S(1)} %fusion.2), channel_id=1, source_target_pairs={{0,120},{8,112},{16,104},{24,96},{32,88},{40,80},{48,72},{56,64},{... | collective-permute-start | bytes 1572872 | tf_op jit(solution)/shard_map/ppermute | solution.py:12
  7.6 0.7 collective-permute-start.30
  8.3 0.0 copy-done.5
  8.3 0.7 fusion.22
  9.6 14.0 %conditional.2 = (bf16[8,8,4096]{2,1,0:T(8,128)(2,1)}) conditional(s32[]{:T(128)} %clamp.7, bf16[8,8,4096]{2,1,0:T(8,128)(2,1)S(1)} %fusion.2, bf16[8,8,4096]{2,1,0:T(8,128)(2,1)S(1)} %fusion.2, bf16[8,8,4096]{2,1,0:T(8,128)(2,1)S(1)} %fusion.2, bf16[8,8,4096]{2,1,0:T(8,128)(2,1)S(1)} %fusion.2, ...), branch_computations={%region_5.6_spmd, %region_6.7_spmd, %region_7.8_spmd, %region_8.9_... | conditional | bytes 2097200 | solution.py:103
  9.6 0.1 collective-permute-start.1
  9.7 13.9 %collective-permute-done.1 = bf16[8,8,4096]{2,1,0:T(8,128)(2,1)} collective-permute-done((bf16[8,8,4096]{2,1,0:T(8,128)(2,1)S(1)}, bf16[8,8,4096]{2,1,0:T(8,128)(2,1)}, u32[]{:S(2)}, u32[]{:S(2)}) %collective-permute-start.1) | collective-permute-done | bytes 524320 | tf_op jit(solution)/shard_map/cond/branch_1_fun/ppermute | solution.py:12
  23.7 1.3 %fusion.25 = (f32[8,8,2048]{2,1,0:T(8,128)S(1)}, f32[8,8,2048]{2,1,0:T(8,128)S(1)}, f32[8,8,2048]{2,1,0:T(8,128)S(1)}, f32[8,8,2048]{2,1,0:T(8,128)S(1)}) fusion(bf16[8,8,4096]{2,1,0:T(8,128)(2,1)} %get-tuple-element.194, bf16[8,8,4096]{2,1,0:T(8,128)(2,1)S(1)} %fusion.2), kind=kLoop, calls=%fused_computation.62 | loop fusion | bytes 4194304 | tf_op jit(solution)/shard_map/slice | solution.py:59
  24.9 0.5 fusion.17
  25.5 0.3 fusion.19
  25.8 4.5 %negate_multiply_fusion = (f32[32,64,512]{2,1,0:T(8,128)}, f32[32,64,512]{2,1,0:T(8,128)}) fusion(f32[64,512]{1,0:T(8,128)S(1)} %get-tuple-element.161, f32[32,512]{1,0:T(8,128)S(1)} %get-tuple-element.159, f32[64,512]{1,0:T(8,128)S(1)} %get-tuple-element.160, f32[32,512]{1,0:T(8,128)S(1)} %get-tuple-element.158), kind=kLoop, calls=%fused_computation.3 | loop fusion | flops 9437184 | bytes 8781824 | tf_op jit(solution)/shard_map/mul | solution.py:49
  31.0 0.0 collective-permute-done.31
  31.0 1.1 %fusion.26 = (f32[8,8,2048]{2,1,0:T(8,128)S(1)}, f32[8,8,2048]{2,1,0:T(8,128)S(1)}) fusion(bf16[8,8,4096]{2,1,0:T(8,128)(2,1)} %collective-permute-done.31), kind=kLoop, calls=%fused_computation.63 | loop fusion | bytes 2097152 | tf_op jit(solution)/shard_map/slice | solution.py:59
  32.1 0.0 collective-permute-done.30
  32.1 0.1 fusion.27
  32.2 4.1 %subtract_reduce_fusion.3 = (f32[8,8,2048]{2,1,0:T(8,128)S(1)}, f32[8,8,2048]{2,1,0:T(8,128)S(1)}, f32[8,8,2048]{2,1,0:T(8,128)S(1)}, f32[8,8,2048]{2,1,0:T(8,12...) fusion(f32[8,8,2048]{2,1,0:T(8,128)S(1)} %get-tuple-element.162, f32[8,8,2048]{2,1,0:T(8,128)S(1)} %get-tuple-element.153, ...), kind=kLoop, calls=%fused_computation.6 | loop fusion | flops 24379392 | bytes 7340032 | tf_op jit(solution)/shard_map/reduce_sum | solution.py:62
  36.3 0.1 pad_maximum_fusion.1
  36.5 0.0 copy-start.2
  36.5 0.1 copy.5
  36.6 0.1 pad_maximum_fusion
  36.7 0.0 copy-start
  36.7 0.1 copy.4
  36.8 1.8 %copy-done.2 = f32[32,64,512]{2,1,0:T(8,128)S(1)} copy-done((f32[32,64,512]{2,1,0:T(8,128)S(1)}, f32[32,64,512]{2,1,0:T(8,128)}, u32[]{:S(2)}) %copy-start.2) | copy-done | bytes 4194328
  38.7 1.9 %fusion.29 = f32[192,512]{1,0:T(8,128)S(1)} fusion(f32[192,2048]{1,0:T(8,128)S(1)} %bitcast.51, f32[2048,512]{1,0:T(8,128)S(1)} %bitcast.48), kind=kOutput, calls=%fused_computation.66 | convolution fusion | flops 1207959552 | bytes 6160384 | tf_op jit(solution)/shard_map/dot_general | solution.py:90
  40.5 0.0 copy-done
  40.6 1.9 %convolution_add_fusion = f32[192,512]{1,0:T(8,128)S(1)} fusion(f32[192,512]{1,0:T(8,128)S(1)} %fusion.29, f32[192,2048]{1,0:T(8,128)S(1)} %bitcast.50, f32[2048,512]{1,0:T(8,128)S(1)} %bitcast.46), kind=kOutput, calls=%fused_computation.13 | convolution fusion | flops 1208057856 | bytes 6553600 | tf_op jit(solution)/shard_map/dot_general | solution.py:91
  42.5 19.3 %conditional.3 = (bf16[8,8,4096]{2,1,0:T(8,128)(2,1)}, f32[24,512]{1,0:T(8,128)S(1)}) conditional(s32[]{:T(128)} %clamp.6, (bf16[8,8,4096]{2,1,0:T(8,128)(2,1)S(1)}, f32[8,24,512]{2,1,0:T(8,128)S(1)}) %tuple.161, (bf16[8,8,4096]{2,1,0:T(8,128)(2,1)S(1)}, f32[8,24,512]{2,1,0:T(8,128)S(1)}) %tuple.162, ...), branch_computations={%region_24.26_spmd, %region_26.28_spmd, %region_28.30_spmd, %regio... | conditional | flops 86016 | bytes 3326012 | solution.py:109
  42.5 0.4 collective-permute-start.26
  42.9 18.3 %all_to_all.76 = f32[8,24,512]{2,1,0:T(8,128)S(1)} all-to-all(f32[8,24,512]{2,1,0:T(8,128)S(1)} %get-tuple-element.119), channel_id=1, replica_groups=mesh['chan'=16,'hour'=8] {'hour'}, dimensions={0} | all-to-all | bytes 786432 | tf_op jit(solution)/shard_map/cond/branch_11_fun/all_to_all | solution.py:97
  61.2 0.5 collective-permute-done.26
  61.8 0.0 copy-start.3
  61.8 1.3 %fusion.24 = (f32[8,8,2048]{2,1,0:T(8,128)S(1)}, f32[8,8,2048]{2,1,0:T(8,128)S(1)}) fusion(bf16[8,8,4096]{2,1,0:T(8,128)(2,1)} %get-tuple-element.129), kind=kLoop, calls=%fused_computation.61 | loop fusion | bytes 2097152 | tf_op jit(solution)/shard_map/slice | solution.py:59
  63.1 0.0 copy-start.1
  63.1 1.4 %subtract_reduce_fusion = (f32[8,8,2048]{2,1,0:T(8,128)S(1)}, f32[8,8,2048]{2,1,0:T(8,128)S(1)}) fusion(f32[8,8,2048]{2,1,0:T(8,128)S(1)} %get-tuple-element.147, f32[8,8,2048]{2,1,0:T(8,128)S(1)} %get-tuple-element.146, f32[8,8,2048]{2,1,0:T(8,128)S(1)} %get-tuple-element.162, f32[8,8,2048]{2,1,0:T(8,128)S(1)} %get-tuple-element.163), kind=kLoop, calls=%fused_computation.1 | loop fusion | flops 8126464 | bytes 3145728 | tf_op jit(solution)/shard_map/reduce_sum | solution.py:62
  64.5 0.0 copy-done.3
  64.5 1.5 %fusion.5 = f32[64,512]{1,0:T(8,128)S(1)} fusion(f32[2048,512]{1,0:T(8,128)S(1)} %bitcast.49, f32[8,8,2048]{2,1,0:T(8,128)S(1)} %get-tuple-element.131), kind=kOutput, calls=%fused_computation.23 | convolution fusion | flops 402653184 | bytes 4849664 | tf_op jit(solution)/shard_map/dot_general | solution.py:90
  66.1 0.0 copy-done.1
  66.1 2.2 %fusion = f32[8,8,512]{2,1,0:T(8,128)} fusion(f32[64,512]{1,0:T(8,128)S(1)} %fusion.5, f32[2048,512]{1,0:T(8,128)S(1)} %bitcast.47, f32[8,8,2048]{2,1,0:T(8,128)S(1)} %get-tuple-element.130), kind=kOutput, calls=%fused_computation.15 | convolution fusion | flops 402685952 | bytes 4980736 | tf_op jit(solution)/shard_map/dot_general | solution.py:91
  68.3 6.6 %all-to-all-start.15 = ((f32[8,8,512]{2,1,0:T(8,128)}), f32[8,8,512]{2,1,0:T(8,128)S(1)}, u32[]{:S(2)}, u32[]{:S(2)}) async-start(f32[8,8,512]{2,1,0:T(8,128)} %fusion), calls=%async_computation.15 | async-start | bytes 262144 | tf_op jit(solution)/shard_map/all_to_all | solution.py:97
  74.9 0.7 broadcast_compare_fusion
  75.6 7.4 %all-to-all-done.15 = f32[8,8,512]{2,1,0:T(8,128)S(1)} async-done(((f32[8,8,512]{2,1,0:T(8,128)}), f32[8,8,512]{2,1,0:T(8,128)S(1)}, u32[]{:S(2)}, u32[]{:S(2)}) %all-to-all-start.15) | async-done | bytes 131104 | tf_op jit(solution)/shard_map/all_to_all | solution.py:97
  83.0 0.6 gather_fusion
  83.6 0.7 bitcast_select_fusion
  (8 shorter events, 0.1 us)
Async XLA Ops:
  0.0 2.8 %copy-start.4 = (bf16[8,8,4096]{2,1,0:T(8,128)(2,1)S(1)}, bf16[8,8,4096]{2,1,0:T(8,128)(2,1)}, u32[]{:S(2)}) copy-start(bf16[8,8,4096]{2,1,0:T(8,128)(2,1)} %param.33) | copy-start | bytes 1572868
  0.0 2.8 %copy-start.6 = (s32[8]{0:T(128)S(1)}, s32[8]{0:T(128)}, u32[]{:S(2)}) copy-start(s32[8]{0:T(128)} %param.34) | copy-start | bytes 100
  1.2 7.1 %copy-start.5 = (s32[4]{0:T(128)S(1)}, s32[4]{0:T(128)}, u32[]{:S(2)}) copy-start(s32[4]{0:T(128)} %param.35) | copy-start | bytes 52
  3.0 28.0 %collective-permute-start.31 = (bf16[8,8,4096]{2,1,0:T(8,128)(2,1)S(1)}, bf16[8,8,4096]{2,1,0:T(8,128)(2,1)}, u32[]{:S(2)}, u32[]{:S(2)}) collective-permute-start(bf16[8,8,4096]{2,1,0:T(8,128)(2,1)S(1)} %fusion.2), channel_id=1, source_target_pairs={{0,120},{8,112},{16,104},{24,96},{32,88},{40,80},{48,72},{56,64},{... | collective-permute-start | bytes 1572872 | tf_op jit(solution)/shard_map/ppermute | solution.py:12
  7.6 24.5 %collective-permute-start.30 = (bf16[8,8,4096]{2,1,0:T(8,128)(2,1)S(1)}, bf16[8,8,4096]{2,1,0:T(8,128)(2,1)S(1)}, u32[]{:S(2)}, u32[]{:S(2)}) collective-permute-start(bf16[8,8,4096]{2,1,0:T(8,128)(2,1)S(1)} %fusion.2), channel_id=1, source_target_pairs={{0,8},{8,0},{16,24},{24,16},{32,40},{40,32},{48,56},{56,48},{64,72... | collective-permute-start | bytes 1572872 | tf_op jit(solution)/shard_map/ppermute | solution.py:12
  9.6 14.0 %collective-permute-start.1 = (bf16[8,8,4096]{2,1,0:T(8,128)(2,1)S(1)}, bf16[8,8,4096]{2,1,0:T(8,128)(2,1)}, u32[]{:S(2)}, u32[]{:S(2)}) collective-permute-start(bf16[8,8,4096]{2,1,0:T(8,128)(2,1)S(1)} %param.1), channel_id=1, source_target_pairs={{0,16},{8,24},{16,0},{24,8},{32,48},{40,56},{48,32},{56,40},{64,80... | collective-permute-start | bytes 1572872 | tf_op jit(solution)/shard_map/cond/branch_1_fun/ppermute | solution.py:12
  36.5 2.2 %copy-start.2 = (f32[32,64,512]{2,1,0:T(8,128)S(1)}, f32[32,64,512]{2,1,0:T(8,128)}, u32[]{:S(2)}) copy-start(f32[32,64,512]{2,1,0:T(8,128)} %get-tuple-element.157) | copy-start | bytes 12582916
  36.7 3.8 %copy-start = (f32[32,64,512]{2,1,0:T(8,128)S(1)}, f32[32,64,512]{2,1,0:T(8,128)}, u32[]{:S(2)}) copy-start(f32[32,64,512]{2,1,0:T(8,128)} %get-tuple-element.156) | copy-start | bytes 12582916
  42.5 19.3 %collective-permute-start.26 = (bf16[8,8,4096]{2,1,0:T(8,128)(2,1)S(1)}, bf16[8,8,4096]{2,1,0:T(8,128)(2,1)}, u32[]{:S(2)}, u32[]{:S(2)}) collective-permute-start(bf16[8,8,4096]{2,1,0:T(8,128)(2,1)S(1)} %get-tuple-element.118), channel_id=1, source_target_pairs={{0,96},{8,104},{16,112},{24,120},{32,64},{40,72},{48,80},{56,88},{... | collective-permute-start | bytes 1572872 | tf_op jit(solution)/shard_map/cond/branch_11_fun/ppermute | solution.py:12
  61.8 2.7 %copy-start.3 = (f32[32,64,512]{2,1,0:T(8,128)S(1)}, f32[32,64,512]{2,1,0:T(8,128)}, u32[]{:S(2)}) copy-start(f32[32,64,512]{2,1,0:T(8,128)} %get-tuple-element.157) | copy-start | bytes 12582916
  63.1 3.0 %copy-start.1 = (f32[32,64,512]{2,1,0:T(8,128)S(1)}, f32[32,64,512]{2,1,0:T(8,128)}, u32[]{:S(2)}) copy-start(f32[32,64,512]{2,1,0:T(8,128)} %get-tuple-element.156) | copy-start | bytes 12582916
  68.3 14.7 %all-to-all-start.15 = ((f32[8,8,512]{2,1,0:T(8,128)}), f32[8,8,512]{2,1,0:T(8,128)S(1)}, u32[]{:S(2)}, u32[]{:S(2)}) async-start(f32[8,8,512]{2,1,0:T(8,128)} %fusion), calls=%async_computation.15 | async-start | bytes 262144 | tf_op jit(solution)/shard_map/all_to_all | solution.py:97
